TPU v7x, 256 devices: a whole 4x4x8 slice. The times are simulated.
256 devices in a mesh: dp: 64 (over x, z, core), mp: 4 (over y).
Axes of the slice: x: 4, y: 4, z: 8, core: 2. Of those that a mesh axis runs over, the one named last changes fastest.
Arguments:
- attn: bfloat16 [2, 4096, 2048], P(None, 'dp', 'mp'), may hold values from -6 to 6
- resid: bfloat16 [2, 4096, 4096], P(None, 'dp', 'mp'), may hold values from -6 to 6
- w_out: bfloat16 [4096, 2048], P('dp', 'mp'), may hold values from -0.125 to 0.125
- gain: float32 [4096], P('mp'), may hold values from 0.1 to 1.9
- neg_owner: int32 [4096, 31], P('dp'), may hold values from 0 to 63, as said below
- neg_local: int32 [4096, 31], P('dp'), may hold values from 0 to 63
Outputs:
- attn_grad: bfloat16 [2, 4096, 2048], P(None, 'dp', 'mp')
- weight_grad: float32 [4096, 2048], P('dp', 'mp')
- gain_grad: float32 [4096], P('mp')
Inputs may be any that keep to these rules, and one draw needn't show every extreme that they name: `neg_owner`: among the 64 queries of one index of dp (aligned blocks of rows), no owner is named more than 62 times, and some owner exactly 62 times.
All inputs are finite; a program needn't handle non-finite values.
Results may differ from a plain program's by a relative error of at most 0.0052.
Values may be sent and summed in bfloat16 or wider, within the bound.
No kernel may reach another device: no remote copies, remote signals or barrier semaphores. Data moves between devices by JAX's collectives and lax.ppermute only.
A program may use at most 128 MiB of HBM per device.

v0:
```python
import jax
import jax.numpy as jnp
from jax import lax
from jax.sharding import PartitionSpec as P

TAU = 0.05
LOSS_SCALE = 32.0
EPS = 1e-06


def shards(attn, resid, w_out, gain, neg_owner, neg_local):
    groups = lax.axis_size("dp")
    pairs_here = attn.shape[1]
    feats = resid.shape[2]
    neg_count = neg_owner.shape[1]
    capacity = 2 * pairs_here * neg_count // groups
    rows_a = attn.reshape(2 * pairs_here, attn.shape[2])
    weight_full = lax.all_gather(w_out, "dp", axis=0, tiled=True)
    proj_part = lax.dot_general(
        rows_a, weight_full, (((1,), (1,)), ((), ())), preferred_element_type=jnp.float32
    )
    proj = lax.psum_scatter(proj_part, "mp", scatter_dimension=1, tiled=True)
    hidden = resid.reshape(2 * pairs_here, feats).astype(jnp.float32) + proj
    normed = hidden * gain
    squares = lax.psum(jnp.sum(normed * normed, axis=1), "mp")
    recip = lax.rsqrt(squares + EPS)[:, None]
    emb = (normed * recip).astype(jnp.bfloat16)
    query = emb[:pairs_here]
    docs = emb[pairs_here:]
    flat_owner = neg_owner.reshape(-1)
    flat_local = neg_local.reshape(-1)
    onehot = (flat_owner[:, None] == jnp.arange(groups, dtype=jnp.int32)[None, :]).astype(jnp.int32)
    ranks = jnp.sum((jnp.cumsum(onehot, axis=0) - 1) * onehot, axis=1)
    slot = flat_owner * capacity + ranks
    request = jnp.full((groups * capacity,), -1, jnp.int32).at[slot].set(flat_local)
    asked = lax.all_to_all(
        request.reshape(groups, capacity), "dp", split_axis=0, concat_axis=0, tiled=True
    )
    valid = asked >= 0
    safe_rows = jnp.maximum(asked, 0)
    outgoing = jnp.where(valid[:, :, None], docs[safe_rows], jnp.zeros((), jnp.bfloat16))
    fetched = lax.all_to_all(outgoing, "dp", split_axis=0, concat_axis=0, tiled=True)
    neg_emb = fetched.reshape(groups * capacity, feats)[slot].reshape(pairs_here, neg_count, feats)
    pos_part = jnp.sum(query.astype(jnp.float32) * docs.astype(jnp.float32), axis=1)
    neg_part = jnp.einsum("pd,pkd->pk", query, neg_emb, preferred_element_type=jnp.float32)
    partial_value = jnp.concatenate([pos_part[:, None], neg_part], axis=1)
    scores = lax.psum(partial_value, "mp") / TAU
    expo = jnp.exp(scores)
    prob = expo / jnp.sum(expo, axis=1, keepdims=True)
    first = (jnp.arange(neg_count + 1) == 0).astype(jnp.float32)[None, :]
    wts = LOSS_SCALE * (prob - first) / TAU
    query_f = query.astype(jnp.float32)
    grad_query = wts[:, 0:1] * docs.astype(jnp.float32) + jnp.einsum(
        "pk,pkd->pd", wts[:, 1:], neg_emb, preferred_element_type=jnp.float32
    )
    terms = (wts[:, 1:, None] * query_f[:, None, :]).astype(jnp.bfloat16)
    slot_buffer = (
        jnp.zeros((groups * capacity, feats), jnp.bfloat16).at[slot].set(terms.reshape(-1, feats))
    )
    returned = lax.all_to_all(
        slot_buffer.reshape(groups, capacity, feats), "dp", split_axis=0, concat_axis=0, tiled=True
    )
    targets = jnp.where(valid, asked, pairs_here).reshape(-1)
    selector = (jnp.arange(pairs_here, dtype=jnp.int32)[:, None] == targets[None, :]).astype(
        jnp.bfloat16
    )
    grad_docs = wts[:, 0:1] * query_f + jnp.dot(
        selector, returned.reshape(-1, feats), preferred_element_type=jnp.float32
    )
    demb = jnp.concatenate([grad_query, grad_docs], axis=0)
    inner = lax.psum(jnp.sum(normed * demb, axis=1), "mp")[:, None]
    dnorm = recip * demb - recip * recip * recip * normed * inner
    gain_grad = lax.psum(jnp.sum(dnorm * hidden, axis=0), "dp")
    dh = (dnorm * gain).astype(jnp.bfloat16)
    dh_full = lax.all_gather(dh, "mp", axis=1, tiled=True)
    attn_grad = (
        jnp.dot(dh_full, weight_full, preferred_element_type=jnp.float32)
        .astype(jnp.bfloat16)
        .reshape(attn.shape)
    )
    weight_grad = lax.psum_scatter(
        lax.dot_general(
            dh_full, rows_a, (((0,), (0,)), ((), ())), preferred_element_type=jnp.float32
        ),
        "dp",
        scatter_dimension=0,
        tiled=True,
    )
    return (attn_grad, weight_grad, gain_grad)


def solution(mesh):
    in_specs = (
        P(None, "dp", "mp"),
        P(None, "dp", "mp"),
        P("dp", "mp"),
        P("mp"),
        P("dp", None),
        P("dp", None),
    )
    out_specs = (P(None, "dp", "mp"), P("dp", "mp"), P("mp"))
    return jax.shard_map(shards, mesh=mesh, in_specs=in_specs, out_specs=out_specs, check_vma=False)
```

profile of v0, /device:TPU:1, one launch (start us, length us, event | category | flops | bytes accessed | tf_op | source)
XLA Modules:
  0.0 858.2 jit_solution(6373866483006717842)
XLA Ops:
  8.0 86.0 %all-gather.3.cloned.1.call-done = bf16[4096,512]{1,0:T(8,128)(2,1)} async-done(((bf16[64,512]{1,0:T(8,128)(2,1)}), bf16[4096,512]{1,0:T(8,128)(2,1)}) %all-gather.3.cloned.1.call-update) | async-done | bytes 4194320 | tf_op jit(solution)/shard_map/all_gather | solution.py:18
  99.6 18.1 %reduce-window.6 = s32[64,16,128]{2,1,0:T(8,128)S(1)} reduce-window(s32[64,16,128]{2,1,0:T(8,128)S(1)} %bitcast.61, s32[]{:T(128)} %constant.16.clone.1), window={size=1x1x128 pad=0_0x0_0x127_0}, to_apply=%region_4.5 | reduce-window | flops 16646144 | bytes 1048580 | tf_op jit(solution)/shard_map/reduce-window
  119.5 10.0 %scatter_custom_fusion = s32[3968]{0:T(1024)S(1)} fusion(s32[1984]{0:T(1024)S(1)} %bitcast.71, s32[1984]{0:T(1024)S(1)} %reshape.152, s32[]{:T(128)} %constant.13.clone.1), kind=kCustom, calls=%fused_computation.49 | custom fusion | bytes 15876 | tf_op jit(solution)/shard_map/scatter | solution.py:35
  129.6 15.3 %all_to_all.22 = s32[64,1,62]{2,1,0:T(1,128)S(1)} all-to-all(s32[64,1,62]{2,1,0:T(1,128)S(1)} %bitcast.67), channel_id=1, replica_groups=mesh['dp'=64,'mp'=4] {'dp'}, dimensions={0} | all-to-all | bytes 31744 | tf_op jit(solution)/shard_map/all_to_all | solution.py:36
  146.3 8.5 psum.28
  156.0 13.3 %gather_fusion = bf16[3968,1024]{1,0:T(8,128)(2,1)} fusion(bf16[64,1024]{1,0:T(8,128)(2,1)S(1)} %get-tuple-element.6, s32[4096]{0:T(1024)S(1)} %pad_clamp_fusion), kind=kCustom, calls=%fused_computation | custom fusion | bytes 16268800 | tf_op jit(solution)/shard_map/gather | solution.py:41
  169.3 9.5 %reshape.133 = bf16[64,62,1024]{2,1,0:T(8,128)(2,1)} reshape(bf16[3968,1024]{1,0:T(8,128)(2,1)} %gather_fusion) | data formatting | bytes 16252928 | tf_op jit(solution)/shard_map/gather | solution.py:41
  178.9 7.2 broadcast_select_fusion
  186.1 7.8 all-to-all-start.1
  198.4 7.1 mul.136
  205.6 174.1 %all-to-all-done.1 = bf16[64,62,1024]{2,1,0:T(8,128)(2,1)} async-done(((bf16[64,62,1024]{2,1,0:T(8,128)(2,1)}), bf16[64,62,1024]{2,1,0:T(8,128)(2,1)}, u32[]{:S(2)}, u32[]{:S(2)}) %all-to-all-start.1) | async-done | bytes 8126496 | tf_op jit(solution)/shard_map/all_to_all | solution.py:42
  379.7 9.6 %reshape.125 = bf16[3968,1024]{1,0:T(8,128)(2,1)} reshape(bf16[64,62,1024]{2,1,0:T(8,128)(2,1)} %all-to-all-done.1) | data formatting | bytes 16252928 | tf_op jit(solution)/shard_map/reshape | solution.py:43
  389.3 15.3 %gather_fusion.1 = bf16[1984,1024]{1,0:T(8,128)(2,1)} fusion(bf16[3968,1024]{1,0:T(8,128)(2,1)} %reshape.125, s32[2048]{0:T(1024)S(1)} %pad_clamp_fusion.1), kind=kCustom, calls=%fused_computation.1 | custom fusion | bytes 8134400 | tf_op jit(solution)/shard_map/gather | solution.py:43
  413.1 11.1 %psum.29 = f32[64,32]{1,0:T(8,128)S(1)} all-reduce(f32[64,32]{1,0:T(8,128)S(1)} %pad_maximum_fusion.1), channel_id=1, replica_groups=mesh['dp'=64,'mp'=4] {'mp'}, use_global_device_ids=true, to_apply=%region_8.9 | all-reduce | flops 2048 | bytes 16384 | tf_op jit(solution)/shard_map/psum | solution.py:47
  424.6 22.3 %scatter_custom_fusion.1 = bf16[3968,1024]{1,0:T(8,128)(2,1)} fusion(s32[1984]{0:T(1024)S(1)} %bitcast.73, f32[1984,1024]{1,0:T(8,128)} %mul.136, f32[1984]{0:T(1024)S(1)} %mul.133, bf16[]{:T(256)} %constant.10.clone.1), kind=kCustom, calls=%fused_computation.6 | custom fusion | flops 4063232 | bytes 16261122 | tf_op jit(solution)/shard_map/scatter | solution.py:58
  446.9 9.6 %reshape.127 = bf16[64,62,1024]{2,1,0:T(8,128)(2,1)} reshape(bf16[3968,1024]{1,0:T(8,128)(2,1)} %scatter_custom_fusion.1) | data formatting | bytes 16252928 | tf_op jit(solution)/shard_map/reshape | solution.py:61
  456.5 9.3 %all-to-all-start.2 = ((bf16[64,62,1024]{2,1,0:T(8,128)(2,1)}), bf16[64,62,1024]{2,1,0:T(8,128)(2,1)}, u32[]{:S(2)}, u32[]{:S(2)}) async-start(bf16[64,62,1024]{2,1,0:T(8,128)(2,1)} %reshape.127), calls=%async_computation.3 | async-start | bytes 16777216 | tf_op jit(solution)/shard_map/all_to_all | solution.py:60
  470.3 181.2 %all-to-all-done.2 = bf16[64,62,1024]{2,1,0:T(8,128)(2,1)} async-done(((bf16[64,62,1024]{2,1,0:T(8,128)(2,1)}), bf16[64,62,1024]{2,1,0:T(8,128)(2,1)}, u32[]{:S(2)}, u32[]{:S(2)}) %all-to-all-start.2) | async-done | bytes 8126496 | tf_op jit(solution)/shard_map/all_to_all | solution.py:60
  651.5 9.6 %reshape.128 = bf16[3968,1024]{1,0:T(8,128)(2,1)} reshape(bf16[64,62,1024]{2,1,0:T(8,128)(2,1)} %all-to-all-done.2) | data formatting | bytes 16252928 | tf_op jit(solution)/shard_map/reshape | solution.py:68
  666.2 7.9 psum.30
  675.1 20.6 %all-gather.5.cloned.1.call-done = bf16[128,4096]{1,0:T(8,128)(2,1)} async-done(((bf16[128,1024]{1,0:T(8,128)(2,1)}), bf16[128,4096]{1,0:T(8,128)(2,1)}) %all-gather.5.cloned.1.call-update) | async-done | bytes 1048592 | tf_op jit(solution)/shard_map/all_gather | solution.py:75
  695.7 5.8 fusion.15
  701.5 127.7 %psum.31 = f32[1024]{0:T(1024)} all-reduce(f32[1024]{0:T(1024)S(1)} %get-tuple-element.3), channel_id=1, replica_groups=mesh['dp'=64,'mp'=4] {'dp'}, use_global_device_ids=true, to_apply=%region_15.16 | all-reduce | flops 1024 | bytes 8192 | tf_op jit(solution)/shard_map/psum | solution.py:73
  832.8 18.9 %reduce-scatter.5.cloned.1.call-done = f32[64,512]{1,0:T(8,128)} async-done(((f32[4096,512]{1,0:T(8,128)}), f32[64,512]{1,0:T(8,128)}) %reduce-scatter.5.cloned.1.call-update) | async-done | bytes 131088 | tf_op jit(solution)/shard_map/reduce_scatter | solution.py:81
  (73 shorter events, 38.4 us)
Async XLA Ops:
  7.2 86.8 %copy-start = (bf16[2,64,512]{2,1,0:T(8,128)(2,1)S(1)}, bf16[2,64,512]{2,1,0:T(8,128)(2,1)}, u32[]{:S(2)}) copy-start(bf16[2,64,512]{2,1,0:T(8,128)(2,1)} %param.6) | copy-start | bytes 393220
  7.2 91.9 %copy-start.5 = (s32[64,31]{0,1:T(8,128)S(1)}, s32[64,31]{0,1:T(8,128)}, u32[]{:S(2)}) copy-start(s32[64,31]{0,1:T(8,128)} %param.10) | copy-start | bytes 23812
  7.2 112.0 %copy-start.6 = (s32[64,31]{0,1:T(8,128)S(1)}, s32[64,31]{0,1:T(8,128)}, u32[]{:S(2)}) copy-start(s32[64,31]{0,1:T(8,128)} %param.11) | copy-start | bytes 23812
  7.2 86.8 %all-gather.3.cloned.1.call-start = ((), (), s32[]{:S(2)}) async-start(), calls=%async_computation.5 | async-start | bytes 4259840 | tf_op jit(solution)/shard_map/all_gather | solution.py:18
  7.9 137.1 %reduce-scatter.3.cloned.1.call-start = ((), (), s32[]{:S(2)}) async-start(), calls=%async_computation.6 | async-start | bytes 2621440 | tf_op jit(solution)/shard_map/reduce_scatter | solution.py:22
  94.0 51.1 %copy-start.3 = (bf16[2,64,1024]{2,1,0:T(8,128)(2,1)S(1)}, bf16[2,64,1024]{2,1,0:T(8,128)(2,1)}, u32[]{:S(2)}) copy-start(bf16[2,64,1024]{2,1,0:T(8,128)(2,1)} %param.7) | copy-start | bytes 786436
  94.0 51.1 %copy-start.4 = (f32[1024]{0:T(1024)S(1)}, f32[1024]{0:T(1024)}, u32[]{:S(2)}) copy-start(f32[1024]{0:T(1024)} %param.9) | copy-start | bytes 12292
  186.1 193.6 %all-to-all-start.1 = ((bf16[64,62,1024]{2,1,0:T(8,128)(2,1)}), bf16[64,62,1024]{2,1,0:T(8,128)(2,1)}, u32[]{:S(2)}, u32[]{:S(2)}) async-start(bf16[64,62,1024]{2,1,0:T(8,128)(2,1)} %broadcast_select_fusion), calls=%async_computation.2 | async-start | bytes 16777216 | tf_op jit(solution)/shard_map/all_to_all | solution.py:42
  456.5 195.1 %all-to-all-start.2 = ((bf16[64,62,1024]{2,1,0:T(8,128)(2,1)}), bf16[64,62,1024]{2,1,0:T(8,128)(2,1)}, u32[]{:S(2)}, u32[]{:S(2)}) async-start(bf16[64,62,1024]{2,1,0:T(8,128)(2,1)} %reshape.127), calls=%async_computation.3 | async-start | bytes 16777216 | tf_op jit(solution)/shard_map/all_to_all | solution.py:60
  465.8 229.9 %all-gather.5.cloned.1.call-start = ((), (), s32[]{:S(2)}) async-start(), calls=%async_computation.7 | async-start | bytes 1310720 | tf_op jit(solution)/shard_map/all_gather | solution.py:75
  661.1 4.9 copy-start.1
  675.1 176.6 %reduce-scatter.5.cloned.1.call-start = ((), (), s32[]{:S(2)}) async-start(), calls=%async_computation.8 | async-start | bytes 8519680 | tf_op jit(solution)/shard_map/reduce_scatter | solution.py:81
  695.7 133.5 %copy-start.2 = (bf16[128,4096]{1,0:T(8,128)(2,1)S(1)}, bf16[128,4096]{1,0:T(8,128)(2,1)}, u32[]{:S(2)}) copy-start(bf16[128,4096]{1,0:T(8,128)(2,1)} %all-gather.5.cloned.1.call-done) | copy-start | bytes 3145732
Sparse Core Ops, SparseCore 0:
  10.8 83.1 all-gather.2
  99.2 29.0 reduce-scatter.2
  675.2 20.4 all-gather.4
  701.7 149.9 reduce-scatter.4
where the time goes:
time: 864 us; the launch traced here: 858 us
  waiting for transfers between devices  482 us (56%)
  blocking collectives  170 us (20%)
  local copies, waits for them, and re-layouts  96.3 us (11%)
  other arithmetic  53.1 us (6%)
  matrix products  25.5 us (3%)
  starting transfers between devices  17.3 us (2%)
  between operations  14.1 us (2%)
    all_to_all x1, waiting for transfers between devices, shards(): lax.all_to_all(slot_buffer.reshape(groups, capacity, feats), 'dp', split_...  181 us
    all_to_all x1, waiting for transfers between devices, shards(): lax.all_to_all(outgoing, 'dp', split_axis=0, concat_axis=0, tiled=True)  174 us
    psum x1, blocking collectives, shards(): gain_grad = lax.psum(jnp.sum(dnorm * hidden, axis=0), 'dp')  128 us
    all_gather x1, waiting for transfers between devices, shards(): weight_full = lax.all_gather(w_out, 'dp', axis=0, tiled=True)  86 us
    gather x2, local copies, waits for them, and re-layouts, shards(): docs[safe_rows]  22.9 us
    scatter x1, other arithmetic, shards(): jnp.zeros((groups * capacity, feats), jnp.bfloat16).at[slot]  22.3 us
    all_gather x1, waiting for transfers between devices, shards(): dh_full = lax.all_gather(dh, 'mp', axis=1, tiled=True)  20.6 us
    reduce_scatter x1, waiting for transfers between devices, shards(): lax.psum_scatter(lax.dot_general(dh_full, rows_a, (((0,), (0,)), ((), ())...  18.9 us
  transfers between devices with their start and end apart: 6, of which 5 were waited for; matrix products, arithmetic and copies ran while one was open for 6% of the time, Pallas kernels for 0%

commit v1 on v0

v1 whole, which is shorter than its diff:
```python
import jax
import jax.numpy as jnp
import numpy as np
from jax import lax
from jax.sharding import Mesh, PartitionSpec as P

TAU = 0.05
LOSS_SCALE = 32.0
EPS = 1e-06
XZ = ("x", "z")
DP = ("x", "z", "c")


def gather_dp(v):
    return lax.all_gather(lax.all_gather(v, XZ, axis=0, tiled=True), "c", axis=0, tiled=True)


def split_bf16(v):
    hi = v.astype(jnp.bfloat16)
    lo = (v - hi.astype(jnp.float32)).astype(jnp.bfloat16)
    return jnp.concatenate([hi, lo], axis=0)


def mm(a, b):
    return jnp.dot(a, b, preferred_element_type=jnp.float32)


def shards(attn, resid, w_out, gain, neg_owner, neg_local):
    n_xz = lax.axis_size("x") * lax.axis_size("z")
    n_c = lax.axis_size("c")
    pairs_here = attn.shape[1]
    heads = attn.shape[2]
    feats = resid.shape[2]
    w_rows = w_out.shape[0]
    total = pairs_here * n_xz * n_c

    pos = ((neg_owner % n_c) * n_xz + neg_owner // n_c) * pairs_here + neg_local
    pos_t = pos.T
    pos_all_t = gather_dp(pos).T

    w_cxz = gather_dp(w_out)
    weight_full = (
        w_cxz.reshape(n_c, n_xz, w_rows, heads).transpose(1, 0, 2, 3).reshape(-1, heads)
    )
    rows_a = attn.reshape(2 * pairs_here, heads)
    proj_part = lax.dot_general(
        rows_a, weight_full, (((1,), (1,)), ((), ())), preferred_element_type=jnp.float32
    )
    proj = lax.psum_scatter(proj_part, "mp", scatter_dimension=1, tiled=True)
    hidden = resid.reshape(2 * pairs_here, feats).astype(jnp.float32) + proj
    normed = hidden * gain
    squares = lax.psum(jnp.sum(normed * normed, axis=1), "mp")
    recip = lax.rsqrt(squares + EPS)[:, None]
    emb = (normed * recip).astype(jnp.bfloat16)
    query = emb[:pairs_here]
    docs = emb[pairs_here:]
    query_f = query.astype(jnp.float32)
    docs_f = docs.astype(jnp.float32)
    q_all = gather_dp(query)
    e_all = gather_dp(docs)

    all_scores = lax.dot_general(
        query, e_all, (((1,), (1,)), ((), ())), preferred_element_type=jnp.float32
    )
    neg_part = jnp.take_along_axis(all_scores, pos, axis=1)
    pos_part = jnp.sum(query_f * docs_f, axis=1)
    partial_value = jnp.concatenate([pos_part[:, None], neg_part], axis=1)
    scores = lax.psum(partial_value, "mp") / TAU
    expo = jnp.exp(scores)
    prob = expo / jnp.sum(expo, axis=1, keepdims=True)
    first = (jnp.arange(scores.shape[1]) == 0).astype(jnp.float32)[None, :]
    wts = LOSS_SCALE * (prob - first) / TAU
    wts_neg_t = wts[:, 1:].T
    wts_all_t = gather_dp(wts[:, 1:]).T

    cols = lax.broadcasted_iota(jnp.int32, (1, 1, total), 2)
    coef_q = jnp.sum(jnp.where(pos_t[:, :, None] == cols, wts_neg_t[:, :, None], 0.0), axis=0)
    both = mm(split_bf16(coef_q), e_all)
    grad_query = wts[:, 0:1] * docs_f + both[:pairs_here] + both[pairs_here:]

    me = lax.axis_index("c") * n_xz + lax.axis_index(XZ)
    own = me * pairs_here + lax.broadcasted_iota(jnp.int32, (1, pairs_here, 1), 1)
    coef_d = jnp.sum(jnp.where(pos_all_t[:, None, :] == own, wts_all_t[:, None, :], 0.0), axis=0)
    both_d = mm(split_bf16(coef_d), q_all)
    grad_docs = wts[:, 0:1] * query_f + both_d[:pairs_here] + both_d[pairs_here:]

    demb = jnp.concatenate([grad_query, grad_docs], axis=0)
    inner = lax.psum(jnp.sum(normed * demb, axis=1), "mp")[:, None]
    dnorm = recip * demb - recip * recip * recip * normed * inner
    gain_grad = lax.psum(jnp.sum(dnorm * hidden, axis=0), DP)
    dh = (dnorm * gain).astype(jnp.bfloat16)
    dh_full = lax.all_gather(dh, "mp", axis=1, tiled=True)
    attn_grad = mm(dh_full, weight_full).astype(jnp.bfloat16).reshape(attn.shape)
    rows = dh_full.shape[0]
    dh_perm = dh_full.reshape(rows, n_xz, n_c, w_rows).transpose(0, 2, 1, 3).reshape(rows, -1)
    wg_part = lax.dot_general(
        dh_perm, rows_a, (((0,), (0,)), ((), ())), preferred_element_type=jnp.float32
    )
    wg_c = lax.psum_scatter(wg_part, "c", scatter_dimension=0, tiled=True)
    weight_grad = lax.psum_scatter(wg_c, XZ, scatter_dimension=0, tiled=True)
    return (attn_grad, weight_grad, gain_grad)


def split_mesh(mesh):
    grid = mesh.devices
    n_dp, n_mp = grid.shape
    column = grid[:, 0]
    n_x = len({d.coords[0] for d in column})
    n_c = len({d.core_on_chip for d in column})
    n_z = n_dp // (n_x * n_c)
    return Mesh(grid.reshape(n_x, n_z, n_c, n_mp), ("x", "z", "c", "mp"))


def solution(mesh):
    inner_mesh = split_mesh(mesh)
    in_specs = (
        P(None, DP, "mp"),
        P(None, DP, "mp"),
        P(DP, "mp"),
        P("mp"),
        P(DP, None),
        P(DP, None),
    )
    out_specs = (P(None, DP, "mp"), P(DP, "mp"), P("mp"))
    return jax.shard_map(
        shards, mesh=inner_mesh, in_specs=in_specs, out_specs=out_specs, check_vma=False
    )
```

time: 864 us -> 784 us (0.907)
  blocking collectives: 170 us -> 259 us
  local copies, waits for them, and re-layouts: 96.3 us -> 24.5 us
  waiting for transfers between devices: 482 us -> 441 us
  other arithmetic: 53.1 us -> 13.8 us
  starting transfers between devices: 17.3 us -> 0.4 us
    all_to_all x2 -> x0, waiting for transfers between devices: 355 us -> none  [the longest x1 181 us: shards(): lax.all_to_all(slot_buffer.reshape(groups, capacity, feats), 'dp', split_...]
    all_gather x1 -> x6, waiting for transfers between devices: 86 us -> 264 us  [the longest x3 240 us: gather_dp(): lax.all_gather(v, XZ, axis=0, tiled=True)]
    all_gather x0 -> x4, blocking collectives: none -> 108 us  [the longest x2 71.2 us: gather_dp(): lax.all_gather(v, XZ, axis=0, tiled=True)]
    reduce_scatter x1 -> x2, waiting for transfers between devices: 18.9 us -> 120 us  [the longest x1 94.8 us: shards(): weight_grad = lax.psum_scatter(wg_c, XZ, scatter_dimension=0, tiled=True)]
    reshape x5 -> x0, local copies, waits for them, and re-layouts: 34 us -> none  [the longest x2 14.7 us: shards(): fetched.reshape(groups * capacity, feats)[slot]]
    reduce_scatter x1, waiting for transfers between devices: 0.02 us -> 32.9 us  [shards(): proj = lax.psum_scatter(proj_part, 'mp', scatter_dimension=1, tiled=True)]
    gather x3, local copies, waits for them, and re-layouts: 38.1 us -> 15.7 us  [shards(): neg_part = jnp.take_along_axis(all_scores, pos, axis=1)]
    scatter x1 -> x0, other arithmetic: 22.3 us -> none  [shards(): jnp.zeros((groups * capacity, feats), jnp.bfloat16).at[slot]]
  transfers between devices with their start and end apart: 6 -> 10, of which waited for: 5 -> 8; matrix products, arithmetic and copies ran while one was open for 6% -> 5% of each run, Pallas kernels for 0% -> 0%
where the time goes in v1:
time: 784 us; the launch traced here: 780 us
  waiting for transfers between devices  441 us (56%)
  blocking collectives  259 us (33%)
  matrix products  26.5 us (3%)
  local copies, waits for them, and re-layouts  24.5 us (3%)
  between operations  14.4 us (2%)
  other arithmetic  13.8 us (2%)
    all_gather x3, waiting for transfers between devices, gather_dp(): lax.all_gather(v, XZ, axis=0, tiled=True)  240 us
    psum x1, blocking collectives, shards(): gain_grad = lax.psum(jnp.sum(dnorm * hidden, axis=0), DP)  125 us
    reduce_scatter x1, waiting for transfers between devices, shards(): weight_grad = lax.psum_scatter(wg_c, XZ, scatter_dimension=0, tiled=True)  94.8 us
    all_gather x2, blocking collectives, gather_dp(): lax.all_gather(v, XZ, axis=0, tiled=True)  71.2 us
    all_gather x2, blocking collectives, gather_dp(): lax.all_gather(lax.all_gather(v, XZ, axis=0, tiled=True), 'c', axis=0, ti...  36.9 us
    reduce_scatter x1, waiting for transfers between devices, shards(): proj = lax.psum_scatter(proj_part, 'mp', scatter_dimension=1, tiled=True)  32.9 us
    reduce_scatter x1, waiting for transfers between devices, shards(): wg_c = lax.psum_scatter(wg_part, 'c', scatter_dimension=0, tiled=True)  25 us
    all_gather x3, waiting for transfers between devices, gather_dp(): lax.all_gather(lax.all_gather(v, XZ, axis=0, tiled=True), 'c', axis=0, ti...  23.4 us
  transfers between devices with their start and end apart: 10, of which 8 were waited for; matrix products, arithmetic and copies ran while one was open for 5% of the time, Pallas kernels for 0%

profile of v1, /device:TPU:1, one launch (start us, length us, event | category | flops | bytes accessed | tf_op | source)
XLA Modules:
  0.0 779.5 jit_solution(2265156428430372609)
XLA Ops:
  8.0 79.7 %all-gather.10.cloned.1.call-done = bf16[2048,512]{1,0:T(8,128)(2,1)} async-done(((bf16[64,512]{1,0:T(8,128)(2,1)}), bf16[2048,512]{1,0:T(8,128)(2,1)}) %all-gather.10.cloned.1.call-update) | async-done | bytes 2097168 | tf_op jit(solution)/shard_map/all_gather | solution.py:15
  87.7 23.3 %all-gather.12.cloned.1.call-done = bf16[4096,512]{1,0:T(8,128)(2,1)} async-done(((bf16[2048,512]{1,0:T(8,128)(2,1)}), bf16[4096,512]{1,0:T(8,128)(2,1)}) %all-gather.12.cloned.1.call-update) | async-done | bytes 4194320 | tf_op jit(solution)/shard_map/all_gather | solution.py:15
  118.6 32.9 %reduce-scatter.4.cloned.1.call-done = f32[128,1024]{1,0:T(8,128)} async-done(((f32[128,4096]{1,0:T(8,128)}), f32[128,1024]{1,0:T(8,128)}) %reduce-scatter.4.cloned.1.call-update) | async-done | bytes 524304 | tf_op jit(solution)/shard_map/reduce_scatter | solution.py:49
  152.8 6.5 psum.28
  161.8 79.2 %all-gather.14.cloned.1.call-done = bf16[2048,1024]{1,0:T(8,128)(2,1)} async-done(((bf16[64,1024]{1,0:T(8,128)(2,1)}), bf16[2048,1024]{1,0:T(8,128)(2,1)}) %all-gather.14.cloned.1.call-update) | async-done | bytes 4194320 | tf_op jit(solution)/shard_map/all_gather | solution.py:15
  241.2 81.5 %all-gather.18.cloned.1.call-done = bf16[2048,1024]{1,0:T(8,128)(2,1)} async-done(((bf16[64,1024]{1,0:T(8,128)(2,1)}), bf16[2048,1024]{1,0:T(8,128)(2,1)}) %all-gather.18.cloned.1.call-update) | async-done | bytes 4194320 | tf_op jit(solution)/shard_map/all_gather | solution.py:15
  323.2 35.6 %all-gather = s32[32,64,31]{1,2,0:T(8,128)S(1)} all-gather(s32[1,64,31]{1,2,0:T(8,128)S(1)} %copy.58), channel_id=1, replica_groups=mesh['x'=4,'z'=8,'c'=2,'mp'=4] {'x','z'}, dimensions={0}, use_global_device_ids=true | all-gather | bytes 261888 | tf_op jit(solution)/shard_map/all_gather | solution.py:15
  359.4 18.9 %all_gather.38 = s32[4096,31]{0,1:T(8,128)S(1)} all-gather(s32[2048,31]{0,1:T(8,128)S(1)} %reshape.77), channel_id=1, replica_groups=mesh['x'=4,'z'=8,'c'=2,'mp'=4] {'c'}, dimensions={0}, use_global_device_ids=true | all-gather | bytes 761856 | tf_op jit(solution)/shard_map/all_gather | solution.py:15
  378.5 6.0 fusion.24
  384.6 15.4 %gather_fusion = f32[1984]{0:T(1024)S(1)} fusion(f32[64,4096]{1,0:T(8,128)S(1)} %fusion.24, s32[1984]{0:T(1024)S(1)} %reshape.65), kind=kCustom, calls=%fused_computation | custom fusion | bytes 31744 | tf_op jit(solution)/shard_map/jit(take_along_axis)/gather | solution.py:65
  400.2 13.3 %psum.29 = f32[64,32]{1,0:T(8,128)S(1)} all-reduce(f32[64,32]{1,0:T(8,128)S(1)} %pad_maximum_fusion.1), channel_id=1, replica_groups=mesh['x'=4,'z'=8,'c'=2,'mp'=4] {'mp'}, use_global_device_ids=true, to_apply=%region_4.5 | all-reduce | flops 2048 | bytes 16384 | tf_op jit(solution)/shard_map/psum | solution.py:68
  414.0 35.6 %all-gather.1 = f32[32,64,31]{1,2,0:T(8,128)S(1)} all-gather(f32[1,64,31]{1,2,0:T(8,128)S(1)} %copy.60), channel_id=1, replica_groups=mesh['x'=4,'z'=8,'c'=2,'mp'=4] {'x','z'}, dimensions={0}, use_global_device_ids=true | all-gather | bytes 261888 | tf_op jit(solution)/shard_map/all_gather | solution.py:15
  450.2 18.0 %all_gather.40 = f32[4096,31]{0,1:T(8,128)S(1)} all-gather(f32[2048,31]{0,1:T(8,128)S(1)} %reshape.79), channel_id=1, replica_groups=mesh['x'=4,'z'=8,'c'=2,'mp'=4] {'c'}, dimensions={0}, use_global_device_ids=true | all-gather | bytes 761856 | tf_op jit(solution)/shard_map/all_gather | solution.py:15
  468.1 5.5 select_reduce_fusion.1
  473.7 4.7 fusion
  478.4 4.0 select_reduce_fusion
  482.5 5.0 fusion.4
  487.9 6.1 psum.30
  495.0 23.2 %all-gather.22.cloned.1.call-done = bf16[128,4096]{1,0:T(8,128)(2,1)} async-done(((bf16[128,1024]{1,0:T(8,128)(2,1)}), bf16[128,4096]{1,0:T(8,128)(2,1)}) %all-gather.22.cloned.1.call-update) | async-done | bytes 1048592 | tf_op jit(solution)/shard_map/all_gather | solution.py:92
  519.9 4.4 fusion.29
  524.4 25.0 %reduce-scatter.6.cloned.1.call-done = f32[2048,512]{1,0:T(8,128)} async-done(((f32[4096,512]{1,0:T(8,128)}), f32[2048,512]{1,0:T(8,128)}) %reduce-scatter.6.cloned.1.call-update) | async-done | bytes 4194320 | tf_op jit(solution)/shard_map/reduce_scatter | solution.py:99
  549.4 124.9 %psum.31 = f32[1024]{0:T(1024)} all-reduce(f32[1024]{0:T(1024)S(1)} %get-tuple-element.9), channel_id=1, replica_groups=mesh['x'=4,'z'=8,'c'=2,'mp'=4] {'x','z','c'}, use_global_device_ids=true, to_apply=%region_13.14 | all-reduce | flops 1024 | bytes 8192 | tf_op jit(solution)/shard_map/psum | solution.py:90
  674.3 3.6 convolution_convert_fusion
  677.9 94.8 %reduce-scatter.8.cloned.1.call-done = f32[64,512]{1,0:T(8,128)} async-done(((f32[2048,512]{1,0:T(8,128)}), f32[64,512]{1,0:T(8,128)}) %reduce-scatter.8.cloned.1.call-update) | async-done | bytes 131088 | tf_op jit(solution)/shard_map/reduce_scatter | solution.py:100
  (74 shorter events, 18.0 us)
Async XLA Ops:
  7.2 106.6 %copy-start = (bf16[2,64,512]{2,1,0:T(8,128)(2,1)S(1)}, bf16[2,64,512]{2,1,0:T(8,128)(2,1)}, u32[]{:S(2)}) copy-start(bf16[2,64,512]{2,1,0:T(8,128)(2,1)} %param.6) | copy-start | bytes 393220
  7.2 80.5 %all-gather.10.cloned.1.call-start = ((), (), s32[]{:S(2)}) async-start(), calls=%async_computation.3 | async-start | bytes 2162688 | tf_op jit(solution)/shard_map/all_gather | solution.py:15
  7.9 103.2 %all-gather.12.cloned.1.call-start = ((), (), s32[]{:S(2)}) async-start(), calls=%async_computation.4 | async-start | bytes 6291456 | tf_op jit(solution)/shard_map/all_gather | solution.py:15
  87.7 63.9 %reduce-scatter.4.cloned.1.call-start = ((), (), s32[]{:S(2)}) async-start(), calls=%async_computation.5 | async-start | bytes 2621440 | tf_op jit(solution)/shard_map/reduce_scatter | solution.py:49
  111.1 40.5 %copy-start.3 = (bf16[2,64,1024]{2,1,0:T(8,128)(2,1)S(1)}, bf16[2,64,1024]{2,1,0:T(8,128)(2,1)}, u32[]{:S(2)}) copy-start(bf16[2,64,1024]{2,1,0:T(8,128)(2,1)} %param.7) | copy-start | bytes 786436
  111.1 40.5 %copy-start.5 = (f32[1024]{0:T(1024)S(1)}, f32[1024]{0:T(1024)}, u32[]{:S(2)}) copy-start(f32[1024]{0:T(1024)} %param.9) | copy-start | bytes 12292
  113.8 1.9 copy-start.1
  115.7 207.0 %copy-start.6 = (s32[64,31]{0,1:T(8,128)S(1)}, s32[64,31]{0,1:T(8,128)}, u32[]{:S(2)}) copy-start(s32[64,31]{0,1:T(8,128)} %param.11) | copy-start | bytes 23812
  115.7 207.1 %copy-start.7 = (s32[64,31]{0,1:T(8,128)S(1)}, s32[64,31]{0,1:T(8,128)}, u32[]{:S(2)}) copy-start(s32[64,31]{0,1:T(8,128)} %param.10) | copy-start | bytes 23812
  118.6 122.5 %all-gather.14.cloned.1.call-start = ((), (), s32[]{:S(2)}) async-start(), calls=%async_computation.6 | async-start | bytes 4325376 | tf_op jit(solution)/shard_map/all_gather | solution.py:15
  161.2 161.4 %all-gather.18.cloned.1.call-start = ((), (), s32[]{:S(2)}) async-start(), calls=%async_computation.8 | async-start | bytes 4325376 | tf_op jit(solution)/shard_map/all_gather | solution.py:15
  161.8 216.8 %all-gather.16.cloned.1.call-start = ((), (), s32[]{:S(2)}) async-start(), calls=%async_computation.7 | async-start | bytes 12582912 | tf_op jit(solution)/shard_map/all_gather | solution.py:15
  241.1 241.4 %all-gather.20.cloned.1.call-start = ((), (), s32[]{:S(2)}) async-start(), calls=%async_computation.9 | async-start | bytes 12582912 | tf_op jit(solution)/shard_map/all_gather | solution.py:15
  322.6 195.5 %all-gather.22.cloned.1.call-start = ((), (), s32[]{:S(2)}) async-start(), calls=%async_computation.10 | async-start | bytes 1310720 | tf_op jit(solution)/shard_map/all_gather | solution.py:92
  482.5 5.2 copy-start.2
  495.0 54.4 %reduce-scatter.6.cloned.1.call-start = ((), (), s32[]{:S(2)}) async-start(), calls=%async_computation.11 | async-start | bytes 12582912 | tf_op jit(solution)/shard_map/reduce_scatter | solution.py:99
  524.3 149.9 %copy-start.4 = (bf16[128,4096]{1,0:T(8,128)(2,1)S(1)}, bf16[128,4096]{1,0:T(8,128)(2,1)}, u32[]{:S(2)}) copy-start(bf16[128,4096]{1,0:T(8,128)(2,1)} %all-gather.22.cloned.1.call-done) | copy-start | bytes 3145732
  524.3 248.3 %reduce-scatter.8.cloned.1.call-start = ((), (), s32[]{:S(2)}) async-start(), calls=%async_computation.12 | async-start | bytes 4325376 | tf_op jit(solution)/shard_map/reduce_scatter | solution.py:100
Sparse Core Ops, SparseCore 0:
  10.6 77.0 all-gather.9
  89.4 21.5 all-gather.11
  118.7 32.7 reduce-scatter.3
  161.3 79.7 all-gather.13
  244.1 78.4 all-gather.17
  324.3 26.2 all-gather.15
  352.3 26.8 all-gather.19
  495.1 23.0 all-gather.21
  524.5 24.8 reduce-scatter.5
  553.7 218.9 reduce-scatter.7

commit v2 on v1

--- a/solution.py
+++ b/solution.py
@@ -11,8 +11,64 @@
 DP = ("x", "z", "c")
 
 
+def ring_collect(v, name, n):
+    if n == 1:
+        return v[None]
+    me = lax.axis_index(name)
+    fwd = [(i, (i + 1) % n) for i in range(n)]
+    bwd = [(i, (i - 1) % n) for i in range(n)]
+    out = jnp.zeros((n,) + v.shape, v.dtype)
+    out = lax.dynamic_update_index_in_dim(out, v, me, 0)
+    if n == 2:
+        return lax.dynamic_update_index_in_dim(out, lax.ppermute(v, name, fwd), 1 - me, 0)
+    n_fwd = n // 2
+    n_bwd = (n - 1) // 2
+    left = right = v
+    for step in range(1, n_fwd + 1):
+        if step > n_bwd:
+            half = v.shape[0] // 2
+            got = jnp.concatenate(
+                [lax.ppermute(left[:half], name, fwd), lax.ppermute(right[half:], name, bwd)], axis=0
+            )
+            out = lax.dynamic_update_index_in_dim(out, got, (me - step) % n, 0)
+            break
+        left = lax.ppermute(left, name, fwd)
+        out = lax.dynamic_update_index_in_dim(out, left, (me - step) % n, 0)
+        right = lax.ppermute(right, name, bwd)
+        out = lax.dynamic_update_index_in_dim(out, right, (me + step) % n, 0)
+    return out
+
+
 def gather_dp(v):
-    return lax.all_gather(lax.all_gather(v, XZ, axis=0, tiled=True), "c", axis=0, tiled=True)
+    gx = ring_collect(v, "x", lax.axis_size("x"))
+    gz = ring_collect(gx, "z", lax.axis_size("z"))
+    return ring_collect(gz, "c", lax.axis_size("c"))
+
+
+def ring_reduce(v, name, n, axis):
+    if n == 1:
+        return v
+    me = lax.axis_index(name)
+    fwd = [(i, (i + 1) % n) for i in range(n)]
+    bwd = [(i, (i - 1) % n) for i in range(n)]
+
+    def block(j):
+        return lax.dynamic_index_in_dim(v, j % n, axis, keepdims=False)
+
+    if n == 2:
+        return block(me) + lax.ppermute(block(me + 1), name, fwd)
+    n_fwd = n // 2
+    n_bwd = (n - 1) // 2
+    acc_f = block(me + n_fwd)
+    for step in range(1, n_fwd + 1):
+        acc_f = lax.ppermute(acc_f, name, fwd) + block(me + n_fwd - step)
+    total = acc_f
+    if n_bwd > 0:
+        acc_b = block(me - n_bwd)
+        for step in range(1, n_bwd):
+            acc_b = lax.ppermute(acc_b, name, bwd) + block(me - n_bwd + step)
+        total = total + lax.ppermute(acc_b, name, bwd)
+    return total
 
 
 def split_bf16(v):
@@ -34,14 +90,16 @@
     w_rows = w_out.shape[0]
     total = pairs_here * n_xz * n_c
 
-    pos = ((neg_owner % n_c) * n_xz + neg_owner // n_c) * pairs_here + neg_local
+    n_x = lax.axis_size("x")
+    n_z = lax.axis_size("z")
+    owner_x = neg_owner // (n_z * n_c)
+    owner_z = (neg_owner // n_c) % n_z
+    owner_c = neg_owner % n_c
+    pos = ((owner_c * n_z + owner_z) * n_x + owner_x) * pairs_here + neg_local
     pos_t = pos.T
-    pos_all_t = gather_dp(pos).T
+    pos_all_t = gather_dp(pos).reshape(total, -1).T
 
-    w_cxz = gather_dp(w_out)
-    weight_full = (
-        w_cxz.reshape(n_c, n_xz, w_rows, heads).transpose(1, 0, 2, 3).reshape(-1, heads)
-    )
+    weight_full = gather_dp(w_out).transpose(2, 1, 0, 3, 4).reshape(-1, heads)
     rows_a = attn.reshape(2 * pairs_here, heads)
     proj_part = lax.dot_general(
         rows_a, weight_full, (((1,), (1,)), ((), ())), preferred_element_type=jnp.float32
@@ -56,8 +114,9 @@
     docs = emb[pairs_here:]
     query_f = query.astype(jnp.float32)
     docs_f = docs.astype(jnp.float32)
-    q_all = gather_dp(query)
-    e_all = gather_dp(docs)
+    emb_all = gather_dp(emb).reshape(n_xz * n_c, 2, pairs_here, feats)
+    q_all = emb_all[:, 0].reshape(total, feats)
+    e_all = emb_all[:, 1].reshape(total, feats)
 
     all_scores = lax.dot_general(
         query, e_all, (((1,), (1,)), ((), ())), preferred_element_type=jnp.float32
@@ -71,14 +130,14 @@
     first = (jnp.arange(scores.shape[1]) == 0).astype(jnp.float32)[None, :]
     wts = LOSS_SCALE * (prob - first) / TAU
     wts_neg_t = wts[:, 1:].T
-    wts_all_t = gather_dp(wts[:, 1:]).T
+    wts_all_t = gather_dp(wts[:, 1:]).reshape(total, -1).T
 
     cols = lax.broadcasted_iota(jnp.int32, (1, 1, total), 2)
     coef_q = jnp.sum(jnp.where(pos_t[:, :, None] == cols, wts_neg_t[:, :, None], 0.0), axis=0)
     both = mm(split_bf16(coef_q), e_all)
     grad_query = wts[:, 0:1] * docs_f + both[:pairs_here] + both[pairs_here:]
 
-    me = lax.axis_index("c") * n_xz + lax.axis_index(XZ)
+    me = (lax.axis_index("c") * n_z + lax.axis_index("z")) * n_x + lax.axis_index("x")
     own = me * pairs_here + lax.broadcasted_iota(jnp.int32, (1, pairs_here, 1), 1)
     coef_d = jnp.sum(jnp.where(pos_all_t[:, None, :] == own, wts_all_t[:, None, :], 0.0), axis=0)
     both_d = mm(split_bf16(coef_d), q_all)
@@ -91,13 +150,12 @@
     dh = (dnorm * gain).astype(jnp.bfloat16)
     dh_full = lax.all_gather(dh, "mp", axis=1, tiled=True)
     attn_grad = mm(dh_full, weight_full).astype(jnp.bfloat16).reshape(attn.shape)
-    rows = dh_full.shape[0]
-    dh_perm = dh_full.reshape(rows, n_xz, n_c, w_rows).transpose(0, 2, 1, 3).reshape(rows, -1)
     wg_part = lax.dot_general(
-        dh_perm, rows_a, (((0,), (0,)), ((), ())), preferred_element_type=jnp.float32
-    )
-    wg_c = lax.psum_scatter(wg_part, "c", scatter_dimension=0, tiled=True)
-    weight_grad = lax.psum_scatter(wg_c, XZ, scatter_dimension=0, tiled=True)
+        dh_full, rows_a, (((0,), (0,)), ((), ())), preferred_element_type=jnp.float32
+    ).reshape(n_x, n_z, n_c, w_rows, heads)
+    wg_xz = ring_reduce(wg_part, "c", n_c, 2)
+    wg_x = ring_reduce(wg_xz, "z", n_z, 1)
+    weight_grad = ring_reduce(wg_x, "x", n_x, 0)
     return (attn_grad, weight_grad, gain_grad)
 
 

time: 784 us -> 634 us (0.81)
  waiting for transfers between devices: 441 us -> 210 us
  starting transfers between devices: 0.4 us -> 118 us
  blocking collectives: 259 us -> 153 us
  local copies, waits for them, and re-layouts: 24.5 us -> 81.7 us
  other arithmetic: 13.8 us -> 23.1 us
    all_gather x6 -> x0, waiting for transfers between devices: 264 us -> none  [the longest x3 240 us: gather_dp(): lax.all_gather(v, XZ, axis=0, tiled=True)]
    ppermute x0 -> x63, waiting for transfers between devices: none -> 152 us  [the longest x16 68.6 us: ring_collect(): left = lax.ppermute(left, name, fwd)]
    reduce_scatter x2 -> x0, waiting for transfers between devices: 120 us -> none  [the longest x1 94.8 us: shards(): weight_grad = lax.psum_scatter(wg_c, XZ, scatter_dimension=0, tiled=True)]
    ppermute x0 -> x63, starting transfers between devices: none -> 118 us  [the longest x16 38.9 us: ring_collect(): right = lax.ppermute(right, name, bwd)]
    all_gather x4 -> x0, blocking collectives: 108 us -> none  [the longest x2 71.2 us: gather_dp(): lax.all_gather(v, XZ, axis=0, tiled=True)]
    dynamic_update_slice x0 -> x51, local copies, waits for them, and re-layouts: none -> 28.5 us  [the longest x12 10.8 us: ring_collect(): out = lax.dynamic_update_index_in_dim(out, v, me, 0)]
    broadcast_in_dim x0 -> x24, local copies, waits for them, and re-layouts: none -> 13.2 us  [the longest x12 12 us: ring_collect(): out = jnp.zeros((n,) + v.shape, v.dtype)]
    slice x1 -> x16, local copies, waits for them, and re-layouts: 0.72 us -> 10.1 us  [the longest x1 9.76 us: shards(): e_all = emb_all[:, 1].reshape(total, feats)]
  transfers between devices with their start and end apart: 10 -> 65, of which waited for: 8 -> 39; matrix products, arithmetic and copies ran while one was open for 5% -> 8% of each run, Pallas kernels for 0% -> 0%
where the time goes in v2:
time: 634 us; the launch traced here: 626 us
  waiting for transfers between devices  210 us (33%)
  blocking collectives  153 us (24%)
  starting transfers between devices  118 us (19%)
  local copies, waits for them, and re-layouts  81.7 us (13%)
  matrix products  24.9 us (4%)
  other arithmetic  23.1 us (4%)
  between operations  15.2 us (2%)
    psum x1, blocking collectives, shards(): gain_grad = lax.psum(jnp.sum(dnorm * hidden, axis=0), DP)  128 us
    ppermute x16, waiting for transfers between devices, ring_collect(): left = lax.ppermute(left, name, fwd)  68.6 us
    ppermute x6, waiting for transfers between devices, ring_reduce(): acc_f = lax.ppermute(acc_f, name, fwd) + block(me + n_fwd - step)  45.5 us
    ppermute x16, starting transfers between devices, ring_collect(): right = lax.ppermute(right, name, bwd)  38.9 us
    reduce_scatter x1, waiting for transfers between devices, shards(): proj = lax.psum_scatter(proj_part, 'mp', scatter_dimension=1, tiled=True)  34 us
    ppermute x4, starting transfers between devices, ring_collect(): lax.ppermute(v, name, fwd)  32.7 us
    all_gather x1, waiting for transfers between devices, shards(): dh_full = lax.all_gather(dh, 'mp', axis=1, tiled=True)  23.9 us
    ppermute x8, starting transfers between devices, ring_collect(): lax.ppermute(right[half:], name, bwd)  22 us
  transfers between devices with their start and end apart: 65, of which 39 were waited for; matrix products, arithmetic and copies ran while one was open for 8% of the time, Pallas kernels for 0%

profile of v2, /device:TPU:1, one launch (start us, length us, event | category | flops | bytes accessed | tf_op | source)
XLA Modules:
  0.0 625.9 jit_solution(10512076295238948063)
XLA Ops:
  46.5 7.6 %collective-permute-start.12 = (bf16[8,4,64,512]{3,2,0,1:T(8,128)(2,1)S(1)}, bf16[8,4,64,512]{3,2,0,1:T(8,128)(2,1)}, u32[]{:S(2)}, u32[]{:S(2)}) collective-permute-start(bf16[8,4,64,512]{3,2,0,1:T(8,128)(2,1)S(1)} %fusion.15), channel_id=1, source_target_pairs={{0,4},{4,0},{1,5},{5,1},{2,6},{6,2},{3,7},{7,3},{8,12},{12,8},{9,1... | collective-permute-start | bytes 6291464 | tf_op jit(solution)/shard_map/ppermute | solution.py:23
  64.9 34.0 %reduce-scatter.2.cloned.1.call-done = f32[128,1024]{0,1:T(8,128)} async-done(((f32[128,4096]{0,1:T(8,128)}), f32[128,1024]{0,1:T(8,128)}) %reduce-scatter.2.cloned.1.call-update) | async-done | bytes 524304 | tf_op jit(solution)/shard_map/reduce_scatter | solution.py:107
  126.6 18.1 %collective-permute-done.17 = bf16[4,128,1024]{2,1,0:T(8,128)(2,1)S(1)} collective-permute-done((bf16[4,128,1024]{2,1,0:T(8,128)(2,1)S(1)}, bf16[4,128,1024]{2,1,0:T(8,128)(2,1)S(1)}, u32[]{:S(2)}, u32[]{:S(2)}) %collective-permute-start.17) | collective-permute-done | bytes 1048608 | tf_op jit(solution)/shard_map/ppermute | solution.py:35
  152.8 13.6 %collective-permute-done.19 = bf16[4,128,1024]{2,1,0:T(8,128)(2,1)S(1)} collective-permute-done((bf16[4,128,1024]{2,1,0:T(8,128)(2,1)S(1)}, bf16[4,128,1024]{2,1,0:T(8,128)(2,1)S(1)}, u32[]{:S(2)}, u32[]{:S(2)}) %collective-permute-start.19) | collective-permute-done | bytes 1048608 | tf_op jit(solution)/shard_map/ppermute | solution.py:35
  173.3 14.6 %collective-permute-done.21 = bf16[4,128,1024]{2,1,0:T(8,128)(2,1)S(1)} collective-permute-done((bf16[4,128,1024]{2,1,0:T(8,128)(2,1)S(1)}, bf16[4,128,1024]{2,1,0:T(8,128)(2,1)S(1)}, u32[]{:S(2)}, u32[]{:S(2)}) %collective-permute-start.21) | collective-permute-done | bytes 1048608 | tf_op jit(solution)/shard_map/ppermute | solution.py:35
  193.0 7.5 %collective-permute-done.23 = bf16[2,128,1024]{2,1,0:T(8,128)(2,1)S(1)} collective-permute-done((bf16[2,128,1024]{2,1,0:T(8,128)(2,1)S(1)}, bf16[2,128,1024]{2,1,0:T(8,128)(2,1)S(1)}, u32[]{:S(2)}, u32[]{:S(2)}) %collective-permute-start.23) | collective-permute-done | bytes 524320 | tf_op jit(solution)/shard_map/ppermute | solution.py:31
  201.5 8.8 %collective-permute-start.25 = (bf16[8,4,128,1024]{3,2,1,0:T(8,128)(2,1)}, bf16[8,4,128,1024]{3,2,1,0:T(8,128)(2,1)}, u32[]{:S(2)}, u32[]{:S(2)}) collective-permute-start(bf16[8,4,128,1024]{3,2,1,0:T(8,128)(2,1)} %fusion), channel_id=1, source_target_pairs={{0,4},{4,0},{1,5},{5,1},{2,6},{6,2},{3,7},{7,3},{8,12},{12,8},{9,1... | collective-permute-start | bytes 25165832 | tf_op jit(solution)/shard_map/ppermute | solution.py:23
  236.8 6.7 %collective-permute-start.38 = (s32[8,4,64,31]{2,1,0,3:T(4,128)S(1)}, s32[8,4,64,31]{2,1,0,3:T(4,128)S(1)}, u32[]{:S(2)}, u32[]{:S(2)}) collective-permute-start(s32[8,4,64,31]{2,1,0,3:T(4,128)S(1)} %fusion.20), channel_id=1, source_target_pairs={{0,4},{4,0},{1,5},{5,1},{2,6},{6,2},{3,7},{7,3},{8,12},{12,8},{9,1... | collective-permute-start | bytes 761864 | tf_op jit(solution)/shard_map/ppermute | solution.py:23
  252.4 8.3 %bitcast_dynamic-update-slice_fusion.1 = bf16[2,8,4,128,1024]{4,3,2,1,0:T(8,128)(2,1)} fusion(bf16[2,8,4,128,1024]{4,3,2,1,0:T(8,128)(2,1)} %broadcast_in_dim.273, s32[]{:T(128)S(6)} %select_n.324, bf16[8,4,128,1024]{3,2,1,0:T(8,128)(2,1)} %fusion), kind=kLoop, calls=%fused_computation.5 | loop fusion | bytes 16777220 | tf_op jit(solution)/shard_map/jit(dynamic_update_index_in_dim)/dynamic_update_slice | solution.py:21
  260.6 8.3 %bitcast_dynamic-update-slice_fusion = bf16[2,8,4,128,1024]{4,3,2,1,0:T(8,128)(2,1)} fusion(bf16[2,8,4,128,1024]{4,3,2,1,0:T(8,128)(2,1)} %bitcast_dynamic-update-slice_fusion.1, s32[]{:T(128)S(6)} %select_n.325, bf16[8,4,128,1024]{3,2,1,0:T(8,128)(2,1)} %collective-permute-done.25), kind=kLoop, calls=%fused_computation.4 | loop fusion | bytes 16777220 | tf_op jit(solution)/shard_map/jit(dynamic_update_index_in_dim)/dynamic_update_slice | solution.py:23
  268.9 9.8 %fusion.38 = (bf16[64,1,64,1024]{3,2,1,0:T(8,128)(2,1)S(1)}, bf16[64,1,64,1024]{3,2,1,0:T(8,128)(2,1)}) fusion(bf16[64,2,64,1024]{3,2,1,0:T(8,128)(2,1)} %bitcast.243), kind=kLoop, calls=%fused_computation.146 | loop fusion | bytes 33554432 | tf_op jit(solution)/shard_map/slice | solution.py:119
  284.7 15.4 %gather_fusion = f32[1984]{0:T(1024)S(1)} fusion(f32[64,4096]{1,0:T(8,128)S(1)} %fusion.16, s32[1984]{0:T(1024)S(1)} %reshape.67), kind=kCustom, calls=%fused_computation | custom fusion | bytes 31744 | tf_op jit(solution)/shard_map/jit(take_along_axis)/gather | solution.py:124
  300.4 11.7 %psum.29 = f32[64,32]{1,0:T(8,128)S(1)} all-reduce(f32[64,32]{1,0:T(8,128)S(1)} %pad_maximum_fusion.1), channel_id=1, replica_groups=mesh['x'=4,'z'=8,'c'=2,'mp'=4] {'mp'}, use_global_device_ids=true, to_apply=%region_4.5 | all-reduce | flops 2048 | bytes 16384 | tf_op jit(solution)/shard_map/psum | solution.py:127
  324.3 6.8 %fusion.1 = f32[128,1024]{0,1:T(8,128)S(1)} fusion(bf16[4096,1024]{1,0:T(8,128)(2,1)} %bitcast.242, bf16[64,4096]{1,0:T(8,128)(2,1)S(1)} %get-tuple-element.3, bf16[64,4096]{1,0:T(8,128)(2,1)S(1)} %get-tuple-element.4), kind=kOutput, calls=%fused_computation.14 | convolution fusion | flops 1075838976 | bytes 9961472 | tf_op jit(solution)/shard_map/dot_general | solution.py:81
  349.6 9.6 %collective-permute-start.51 = (f32[8,4,64,31]{2,1,0,3:T(4,128)S(1)}, f32[8,4,64,31]{2,1,0,3:T(4,128)S(1)}, u32[]{:S(2)}, u32[]{:S(2)}) collective-permute-start(f32[8,4,64,31]{2,1,0,3:T(4,128)S(1)} %fusion.21), channel_id=1, source_target_pairs={{0,4},{4,0},{1,5},{5,1},{2,6},{6,2},{3,7},{7,3},{8,12},{12,8},{9,1... | collective-permute-start | bytes 761864 | tf_op jit(solution)/shard_map/ppermute | solution.py:23
  365.7 6.8 %fusion.5 = f32[128,1024]{0,1:T(8,128)S(1)} fusion(bf16[4096,1024]{1,0:T(8,128)(2,1)} %bitcast.246, bf16[64,4096]{1,0:T(8,128)(2,1)S(1)} %get-tuple-element.5, bf16[64,4096]{1,0:T(8,128)(2,1)S(1)} %get-tuple-element.6), kind=kOutput, calls=%fused_computation.18 | convolution fusion | flops 1075838976 | bytes 9961472 | tf_op jit(solution)/shard_map/dot_general | solution.py:81
  373.2 6.8 %psum.30 = f32[128]{0:T(128)S(1)} all-reduce(f32[128]{0:T(128)S(1)} %multiply_reduce_fusion.1), channel_id=1, replica_groups=mesh['x'=4,'z'=8,'c'=2,'mp'=4] {'mp'}, use_global_device_ids=true, to_apply=%region_9.10 | all-reduce | flops 128 | bytes 1024 | tf_op jit(solution)/shard_map/psum | solution.py:147
  381.2 23.9 %all-gather.2.cloned.1.call-done = bf16[128,4096]{0,1:T(8,128)(2,1)} async-done(((bf16[128,1024]{0,1:T(8,128)(2,1)}), bf16[128,4096]{0,1:T(8,128)(2,1)}) %all-gather.2.cloned.1.call-update) | async-done | bytes 1048592 | tf_op jit(solution)/shard_map/all_gather | solution.py:151
  416.2 7.1 %collective-permute-done.52 = f32[4,8,64,512]{3,2,1,0:T(8,128)} collective-permute-done((f32[4,8,64,512]{3,2,1,0:T(8,128)}, f32[4,8,64,512]{3,2,1,0:T(8,128)}, u32[]{:S(2)}, u32[]{:S(2)}) %collective-permute-start.52) | collective-permute-done | bytes 4194336 | tf_op jit(solution)/shard_map/ppermute | solution.py:59
  431.2 11.8 %collective-permute-done.53 = f32[4,64,512]{2,1,0:T(8,128)S(1)} collective-permute-done((f32[4,64,512]{2,1,0:T(8,128)S(1)}, f32[4,64,512]{2,1,0:T(8,128)S(1)}, u32[]{:S(2)}, u32[]{:S(2)}) %collective-permute-start.53) | collective-permute-done | bytes 524320 | tf_op jit(solution)/shard_map/ppermute | solution.py:64
  443.2 13.7 %collective-permute-done.54 = f32[4,64,512]{2,1,0:T(8,128)S(1)} collective-permute-done((f32[4,64,512]{2,1,0:T(8,128)S(1)}, f32[4,64,512]{2,1,0:T(8,128)S(1)}, u32[]{:S(2)}, u32[]{:S(2)}) %collective-permute-start.54) | collective-permute-done | bytes 524320 | tf_op jit(solution)/shard_map/ppermute | solution.py:64
  459.9 10.2 %collective-permute-done.55 = f32[4,64,512]{2,1,0:T(8,128)S(1)} collective-permute-done((f32[4,64,512]{2,1,0:T(8,128)S(1)}, f32[4,64,512]{2,1,0:T(8,128)S(1)}, u32[]{:S(2)}, u32[]{:S(2)}) %collective-permute-start.55) | collective-permute-done | bytes 524320 | tf_op jit(solution)/shard_map/ppermute | solution.py:64
  473.1 9.4 %collective-permute-done.56 = f32[4,64,512]{2,1,0:T(8,128)S(1)} collective-permute-done((f32[4,64,512]{2,1,0:T(8,128)S(1)}, f32[4,64,512]{2,1,0:T(8,128)S(1)}, u32[]{:S(2)}, u32[]{:S(2)}) %collective-permute-start.56) | collective-permute-done | bytes 524320 | tf_op jit(solution)/shard_map/ppermute | solution.py:64
  484.9 127.8 %psum.31 = f32[1024]{0:T(1024)} all-reduce(f32[1024]{0:T(1024)S(1)} %get-tuple-element.19), channel_id=1, replica_groups=mesh['x'=4,'z'=8,'c'=2,'mp'=4] {'x','z','c'}, use_global_device_ids=true, to_apply=%region_11.12 | all-reduce | flops 1024 | bytes 8192 | tf_op jit(solution)/shard_map/psum | solution.py:149
  (286 shorter events, 212.5 us)
Async XLA Ops:
  7.2 91.7 %reduce-scatter.2.cloned.1.call-start = ((), (), s32[]{:S(2)}) async-start(), calls=%async_computation.1 | async-start | bytes 2621440 | tf_op jit(solution)/shard_map/reduce_scatter | solution.py:107
  46.5 11.5 %collective-permute-start.12 = (bf16[8,4,64,512]{3,2,0,1:T(8,128)(2,1)S(1)}, bf16[8,4,64,512]{3,2,0,1:T(8,128)(2,1)}, u32[]{:S(2)}, u32[]{:S(2)}) collective-permute-start(bf16[8,4,64,512]{3,2,0,1:T(8,128)(2,1)S(1)} %fusion.15), channel_id=1, source_target_pairs={{0,4},{4,0},{1,5},{5,1},{2,6},{6,2},{3,7},{7,3},{8,12},{12,8},{9,1... | collective-permute-start | bytes 6291464 | tf_op jit(solution)/shard_map/ppermute | solution.py:23
  64.6 340.4 %all-gather.2.cloned.1.call-start = ((), (), s32[]{:S(2)}) async-start(), calls=%async_computation.2 | async-start | bytes 1310720 | tf_op jit(solution)/shard_map/all_gather | solution.py:151
  123.4 21.3 %collective-permute-start.17 = (bf16[4,128,1024]{2,1,0:T(8,128)(2,1)S(1)}, bf16[4,128,1024]{2,1,0:T(8,128)(2,1)S(1)}, u32[]{:S(2)}, u32[]{:S(2)}) collective-permute-start(bf16[4,128,1024]{2,1,0:T(8,128)(2,1)S(1)} %constant_dynamic-update-slice_fusion), channel_id=1, source_target_pairs={{0,8},{8,16},{16,24},{24,32},{32,40},{40,48},{48,56},{56,0},{1,9},... | collective-permute-start | bytes 3145736 | tf_op jit(solution)/shard_map/ppermute | solution.py:35
  124.7 20.0 %collective-permute-start.18 = (bf16[4,128,1024]{2,1,0:T(8,128)(2,1)S(1)}, bf16[4,128,1024]{2,1,0:T(8,128)(2,1)S(1)}, u32[]{:S(2)}, u32[]{:S(2)}) collective-permute-start(bf16[4,128,1024]{2,1,0:T(8,128)(2,1)S(1)} %constant_dynamic-update-slice_fusion), channel_id=1, source_target_pairs={{0,56},{8,0},{16,8},{24,16},{32,24},{40,32},{48,40},{56,48},{1,57}... | collective-permute-start | bytes 3145736 | tf_op jit(solution)/shard_map/ppermute | solution.py:37
  144.7 21.6 %collective-permute-start.19 = (bf16[4,128,1024]{2,1,0:T(8,128)(2,1)S(1)}, bf16[4,128,1024]{2,1,0:T(8,128)(2,1)S(1)}, u32[]{:S(2)}, u32[]{:S(2)}) collective-permute-start(bf16[4,128,1024]{2,1,0:T(8,128)(2,1)S(1)} %collective-permute-done.17), channel_id=1, source_target_pairs={{0,8},{8,16},{16,24},{24,32},{32,40},{40,48},{48,56},{56,0},{1,9},... | collective-permute-start | bytes 3145736 | tf_op jit(solution)/shard_map/ppermute | solution.py:35
  144.7 21.6 %collective-permute-start.20 = (bf16[4,128,1024]{2,1,0:T(8,128)(2,1)S(1)}, bf16[4,128,1024]{2,1,0:T(8,128)(2,1)S(1)}, u32[]{:S(2)}, u32[]{:S(2)}) collective-permute-start(bf16[4,128,1024]{2,1,0:T(8,128)(2,1)S(1)} %collective-permute-done.18), channel_id=1, source_target_pairs={{0,56},{8,0},{16,8},{24,16},{32,24},{40,32},{48,40},{56,48},{1,57}... | collective-permute-start | bytes 3145736 | tf_op jit(solution)/shard_map/ppermute | solution.py:37
  166.3 21.6 %collective-permute-start.21 = (bf16[4,128,1024]{2,1,0:T(8,128)(2,1)S(1)}, bf16[4,128,1024]{2,1,0:T(8,128)(2,1)S(1)}, u32[]{:S(2)}, u32[]{:S(2)}) collective-permute-start(bf16[4,128,1024]{2,1,0:T(8,128)(2,1)S(1)} %collective-permute-done.19), channel_id=1, source_target_pairs={{0,8},{8,16},{16,24},{24,32},{32,40},{40,48},{48,56},{56,0},{1,9},... | collective-permute-start | bytes 3145736 | tf_op jit(solution)/shard_map/ppermute | solution.py:35
  166.3 21.7 %collective-permute-start.22 = (bf16[4,128,1024]{2,1,0:T(8,128)(2,1)S(1)}, bf16[4,128,1024]{2,1,0:T(8,128)(2,1)S(1)}, u32[]{:S(2)}, u32[]{:S(2)}) collective-permute-start(bf16[4,128,1024]{2,1,0:T(8,128)(2,1)S(1)} %collective-permute-done.20), channel_id=1, source_target_pairs={{0,56},{8,0},{16,8},{24,16},{32,24},{40,32},{48,40},{56,48},{1,57}... | collective-permute-start | bytes 3145736 | tf_op jit(solution)/shard_map/ppermute | solution.py:37
  188.0 12.5 %collective-permute-start.23 = (bf16[2,128,1024]{2,1,0:T(8,128)(2,1)S(1)}, bf16[2,128,1024]{2,1,0:T(8,128)(2,1)S(1)}, u32[]{:S(2)}, u32[]{:S(2)}) collective-permute-start(bf16[2,128,1024]{2,1,0:T(8,128)(2,1)S(1)} %slice.116), channel_id=1, source_target_pairs={{0,8},{8,16},{16,24},{24,32},{32,40},{40,48},{48,56},{56,0},{1,9},... | collective-permute-start | bytes 1572872 | tf_op jit(solution)/shard_map/ppermute | solution.py:31
  188.1 12.4 %collective-permute-start.24 = (bf16[2,128,1024]{2,1,0:T(8,128)(2,1)S(1)}, bf16[2,128,1024]{2,1,0:T(8,128)(2,1)S(1)}, u32[]{:S(2)}, u32[]{:S(2)}) collective-permute-start(bf16[2,128,1024]{2,1,0:T(8,128)(2,1)S(1)} %slice.117), channel_id=1, source_target_pairs={{0,56},{8,0},{16,8},{24,16},{32,24},{40,32},{48,40},{56,48},{1,57}... | collective-permute-start | bytes 1572872 | tf_op jit(solution)/shard_map/ppermute | solution.py:31
  201.5 59.1 %collective-permute-start.25 = (bf16[8,4,128,1024]{3,2,1,0:T(8,128)(2,1)}, bf16[8,4,128,1024]{3,2,1,0:T(8,128)(2,1)}, u32[]{:S(2)}, u32[]{:S(2)}) collective-permute-start(bf16[8,4,128,1024]{3,2,1,0:T(8,128)(2,1)} %fusion), channel_id=1, source_target_pairs={{0,4},{4,0},{1,5},{5,1},{2,6},{6,2},{3,7},{7,3},{8,12},{12,8},{9,1... | collective-permute-start | bytes 25165832 | tf_op jit(solution)/shard_map/ppermute | solution.py:23
  321.6 10.1 %collective-permute-start.41 = (f32[32,31]{1,0:T(8,128)S(1)}, f32[32,31]{1,0:T(8,128)S(1)}, u32[]{:S(2)}, u32[]{:S(2)}) collective-permute-start(f32[32,31]{1,0:T(8,128)S(1)} %slice.127), channel_id=1, source_target_pairs={{0,64},{64,128},{128,192},{192,0},{1,65},{65,129},{129,193},{193,1... | collective-permute-start | bytes 11912 | tf_op jit(solution)/shard_map/ppermute | solution.py:31
  321.7 10.0 %collective-permute-start.42 = (f32[32,31]{1,0:T(8,128)S(1)}, f32[32,31]{1,0:T(8,128)S(1)}, u32[]{:S(2)}, u32[]{:S(2)}) collective-permute-start(f32[32,31]{1,0:T(8,128)S(1)} %slice.128), channel_id=1, source_target_pairs={{0,192},{64,0},{128,64},{192,128},{1,193},{65,1},{129,65},{193,129... | collective-permute-start | bytes 11912 | tf_op jit(solution)/shard_map/ppermute | solution.py:31
  349.6 11.1 %collective-permute-start.51 = (f32[8,4,64,31]{2,1,0,3:T(4,128)S(1)}, f32[8,4,64,31]{2,1,0,3:T(4,128)S(1)}, u32[]{:S(2)}, u32[]{:S(2)}) collective-permute-start(f32[8,4,64,31]{2,1,0,3:T(4,128)S(1)} %fusion.21), channel_id=1, source_target_pairs={{0,4},{4,0},{1,5},{5,1},{2,6},{6,2},{3,7},{7,3},{8,12},{12,8},{9,1... | collective-permute-start | bytes 761864 | tf_op jit(solution)/shard_map/ppermute | solution.py:23
  413.3 10.0 %collective-permute-start.52 = (f32[4,8,64,512]{3,2,1,0:T(8,128)}, f32[4,8,64,512]{3,2,1,0:T(8,128)}, u32[]{:S(2)}, u32[]{:S(2)}) collective-permute-start(f32[4,8,64,512]{3,2,1,0:T(8,128)} %dynamic-slice_bitcast_fusion), channel_id=1, source_target_pairs={{0,4},{4,0},{1,5},{5,1},{2,6},{6,2},{3,7},{7,3},{8,12},{12,8},{9,1... | collective-permute-start | bytes 12582920 | tf_op jit(solution)/shard_map/ppermute | solution.py:59
  427.9 15.0 %collective-permute-start.53 = (f32[4,64,512]{2,1,0:T(8,128)S(1)}, f32[4,64,512]{2,1,0:T(8,128)S(1)}, u32[]{:S(2)}, u32[]{:S(2)}) collective-permute-start(f32[4,64,512]{2,1,0:T(8,128)S(1)} %get-tuple-element.17), channel_id=1, source_target_pairs={{0,8},{8,16},{16,24},{24,32},{32,40},{40,48},{48,56},{56,0},{1,9},... | collective-permute-start | bytes 1572872 | tf_op jit(solution)/shard_map/ppermute | solution.py:64
  429.3 13.9 %collective-permute-start.57 = (f32[4,64,512]{2,1,0:T(8,128)S(1)}, f32[4,64,512]{2,1,0:T(8,128)S(1)}, u32[]{:S(2)}, u32[]{:S(2)}) collective-permute-start(f32[4,64,512]{2,1,0:T(8,128)S(1)} %get-tuple-element.18), channel_id=1, source_target_pairs={{0,56},{8,0},{16,8},{24,16},{32,24},{40,32},{48,40},{56,48},{1,57}... | collective-permute-start | bytes 1572872 | tf_op jit(solution)/shard_map/ppermute | solution.py:69
  443.1 13.8 %collective-permute-start.54 = (f32[4,64,512]{2,1,0:T(8,128)S(1)}, f32[4,64,512]{2,1,0:T(8,128)S(1)}, u32[]{:S(2)}, u32[]{:S(2)}) collective-permute-start(f32[4,64,512]{2,1,0:T(8,128)S(1)} %bitcast_add_fusion.6), channel_id=1, source_target_pairs={{0,8},{8,16},{16,24},{24,32},{32,40},{40,48},{48,56},{56,0},{1,9},... | collective-permute-start | bytes 1572872 | tf_op jit(solution)/shard_map/ppermute | solution.py:64
  457.1 13.0 %collective-permute-start.55 = (f32[4,64,512]{2,1,0:T(8,128)S(1)}, f32[4,64,512]{2,1,0:T(8,128)S(1)}, u32[]{:S(2)}, u32[]{:S(2)}) collective-permute-start(f32[4,64,512]{2,1,0:T(8,128)S(1)} %get-tuple-element.15), channel_id=1, source_target_pairs={{0,8},{8,16},{16,24},{24,32},{32,40},{40,48},{48,56},{56,0},{1,9},... | collective-permute-start | bytes 1572872 | tf_op jit(solution)/shard_map/ppermute | solution.py:64
  457.2 12.9 %collective-permute-start.58 = (f32[4,64,512]{2,1,0:T(8,128)S(1)}, f32[4,64,512]{2,1,0:T(8,128)S(1)}, u32[]{:S(2)}, u32[]{:S(2)}) collective-permute-start(f32[4,64,512]{2,1,0:T(8,128)S(1)} %get-tuple-element.16), channel_id=1, source_target_pairs={{0,56},{8,0},{16,8},{24,16},{32,24},{40,32},{48,40},{56,48},{1,57}... | collective-permute-start | bytes 1572872 | tf_op jit(solution)/shard_map/ppermute | solution.py:69
  470.3 12.1 %collective-permute-start.56 = (f32[4,64,512]{2,1,0:T(8,128)S(1)}, f32[4,64,512]{2,1,0:T(8,128)S(1)}, u32[]{:S(2)}, u32[]{:S(2)}) collective-permute-start(f32[4,64,512]{2,1,0:T(8,128)S(1)} %get-tuple-element.13), channel_id=1, source_target_pairs={{0,8},{8,16},{16,24},{24,32},{32,40},{40,48},{48,56},{56,0},{1,9},... | collective-permute-start | bytes 1572872 | tf_op jit(solution)/shard_map/ppermute | solution.py:64
  470.4 12.0 %collective-permute-start.59 = (f32[4,64,512]{2,1,0:T(8,128)S(1)}, f32[4,64,512]{2,1,0:T(8,128)S(1)}, u32[]{:S(2)}, u32[]{:S(2)}) collective-permute-start(f32[4,64,512]{2,1,0:T(8,128)S(1)} %get-tuple-element.14), channel_id=1, source_target_pairs={{0,56},{8,0},{16,8},{24,16},{32,24},{40,32},{48,40},{56,48},{1,57}... | collective-permute-start | bytes 1572872 | tf_op jit(solution)/shard_map/ppermute | solution.py:70
  483.7 129.0 %collective-permute-start.60 = (f32[64,512]{1,0:T(8,128)S(1)}, f32[64,512]{1,0:T(8,128)S(1)}, u32[]{:S(2)}, u32[]{:S(2)}) collective-permute-start(f32[64,512]{1,0:T(8,128)S(1)} %get-tuple-element.21), channel_id=1, source_target_pairs={{0,64},{64,128},{128,192},{192,0},{1,65},{65,129},{129,193},{193,1... | collective-permute-start | bytes 393224 | tf_op jit(solution)/shard_map/ppermute | solution.py:64
  (54 other events, 762.6 us)
Sparse Core Ops, SparseCore 0:
  64.7 34.1 reduce-scatter.1
  381.3 23.7 all-gather.1

commit v3 on v2

--- a/solution.py
+++ b/solution.py
@@ -71,6 +71,10 @@
     return total
 
 
+def ring_sum(v, name):
+    return jnp.sum(ring_collect(v, name, lax.axis_size(name)), axis=0)
+
+
 def split_bf16(v):
     hi = v.astype(jnp.bfloat16)
     lo = (v - hi.astype(jnp.float32)).astype(jnp.bfloat16)
@@ -104,10 +108,11 @@
     proj_part = lax.dot_general(
         rows_a, weight_full, (((1,), (1,)), ((), ())), preferred_element_type=jnp.float32
     )
-    proj = lax.psum_scatter(proj_part, "mp", scatter_dimension=1, tiled=True)
+    n_mp = lax.axis_size("mp")
+    proj = ring_reduce(proj_part.reshape(proj_part.shape[0], n_mp, feats), "mp", n_mp, 1)
     hidden = resid.reshape(2 * pairs_here, feats).astype(jnp.float32) + proj
     normed = hidden * gain
-    squares = lax.psum(jnp.sum(normed * normed, axis=1), "mp")
+    squares = ring_sum(jnp.sum(normed * normed, axis=1), "mp")
     recip = lax.rsqrt(squares + EPS)[:, None]
     emb = (normed * recip).astype(jnp.bfloat16)
     query = emb[:pairs_here]
@@ -124,7 +129,7 @@
     neg_part = jnp.take_along_axis(all_scores, pos, axis=1)
     pos_part = jnp.sum(query_f * docs_f, axis=1)
     partial_value = jnp.concatenate([pos_part[:, None], neg_part], axis=1)
-    scores = lax.psum(partial_value, "mp") / TAU
+    scores = ring_sum(partial_value, "mp") / TAU
     expo = jnp.exp(scores)
     prob = expo / jnp.sum(expo, axis=1, keepdims=True)
     first = (jnp.arange(scores.shape[1]) == 0).astype(jnp.float32)[None, :]
@@ -144,11 +149,11 @@
     grad_docs = wts[:, 0:1] * query_f + both_d[:pairs_here] + both_d[pairs_here:]
 
     demb = jnp.concatenate([grad_query, grad_docs], axis=0)
-    inner = lax.psum(jnp.sum(normed * demb, axis=1), "mp")[:, None]
+    inner = ring_sum(jnp.sum(normed * demb, axis=1), "mp")[:, None]
     dnorm = recip * demb - recip * recip * recip * normed * inner
-    gain_grad = lax.psum(jnp.sum(dnorm * hidden, axis=0), DP)
+    gain_grad = jnp.sum(gather_dp(jnp.sum(dnorm * hidden, axis=0)), axis=(0, 1, 2))
     dh = (dnorm * gain).astype(jnp.bfloat16)
-    dh_full = lax.all_gather(dh, "mp", axis=1, tiled=True)
+    dh_full = ring_collect(dh, "mp", n_mp).transpose(1, 0, 2).reshape(dh.shape[0], -1)
     attn_grad = mm(dh_full, weight_full).astype(jnp.bfloat16).reshape(attn.shape)
     wg_part = lax.dot_general(
         dh_full, rows_a, (((0,), (0,)), ((), ())), preferred_element_type=jnp.float32

time: 634 us -> 504 us (0.79)
  blocking collectives: 153 us -> 0 us
  starting transfers between devices: 118 us -> 172 us
  waiting for transfers between devices: 210 us -> 190 us
  between operations: 15.2 us -> 2.22 us
    psum x4 -> x0, blocking collectives: 153 us -> none  [the longest x1 128 us: shards(): gain_grad = lax.psum(jnp.sum(dnorm * hidden, axis=0), DP)]
    reduce_scatter x1 -> x0, waiting for transfers between devices: 34 us -> none  [shards(): proj = lax.psum_scatter(proj_part, 'mp', scatter_dimension=1, tiled=True)]
    all_gather x1 -> x0, waiting for transfers between devices: 23.9 us -> none  [shards(): dh_full = lax.all_gather(dh, 'mp', axis=1, tiled=True)]
    ppermute x16 -> x24, starting transfers between devices: 38.9 us -> 61.9 us  [ring_collect(): right = lax.ppermute(right, name, bwd)]
    ppermute x6 -> x8, waiting for transfers between devices: 45.5 us -> 65.5 us  [ring_reduce(): acc_f = lax.ppermute(acc_f, name, fwd) + block(me + n_fwd - step)]
    ppermute x8 -> x14, starting transfers between devices: 22 us -> 37.8 us  [ring_collect(): lax.ppermute(right[half:], name, bwd)]
    ppermute x8 -> x14, waiting for transfers between devices: 17.6 us -> 28.9 us  [ring_collect(): lax.ppermute(left[:half], name, fwd)]
    ppermute x16 -> x24, waiting for transfers between devices: 68.6 us -> 79.6 us  [ring_collect(): left = lax.ppermute(left, name, fwd)]
  transfers between devices with their start and end apart: 65 -> 95, of which waited for: 39 -> 48; matrix products, arithmetic and copies ran while one was open for 8% -> 19% of each run, Pallas kernels for 0% -> 0%
where the time goes in v3:
time: 504 us; the launch traced here: 495 us
  waiting for transfers between devices  190 us (38%)
  starting transfers between devices  172 us (34%)
  local copies, waits for them, and re-layouts  86.6 us (17%)
  other arithmetic  26.3 us (5%)
  matrix products  19 us (4%)
    ppermute x24, waiting for transfers between devices, ring_collect(): left = lax.ppermute(left, name, fwd)  79.6 us
    ppermute x8, waiting for transfers between devices, ring_reduce(): acc_f = lax.ppermute(acc_f, name, fwd) + block(me + n_fwd - step)  65.5 us
    ppermute x24, starting transfers between devices, ring_collect(): right = lax.ppermute(right, name, bwd)  61.9 us
    ppermute x5, starting transfers between devices, ring_collect(): lax.ppermute(v, name, fwd)  40.4 us
    ppermute x14, starting transfers between devices, ring_collect(): lax.ppermute(right[half:], name, bwd)  37.8 us
    ppermute x14, waiting for transfers between devices, ring_collect(): lax.ppermute(left[:half], name, fwd)  28.9 us
    gather x3, local copies, waits for them, and re-layouts, shards(): neg_part = jnp.take_along_axis(all_scores, pos, axis=1)  15.7 us
    dot_general x3, matrix products, mm(): return jnp.dot(a, b, preferred_element_type=jnp.float32)  13.9 us
  transfers between devices with their start and end apart: 95, of which 48 were waited for; matrix products, arithmetic and copies ran while one was open for 19% of the time, Pallas kernels for 0%

profile of v3, /device:TPU:1, one launch (start us, length us, event | category | flops | bytes accessed | tf_op | source)
XLA Modules:
  0.0 495.5 jit_solution(11494086776774977955)
XLA Ops:
  39.9 7.4 %collective-permute-start.12 = (bf16[8,4,64,512]{3,2,0,1:T(8,128)(2,1)S(1)}, bf16[8,4,64,512]{3,2,0,1:T(8,128)(2,1)}, u32[]{:S(2)}, u32[]{:S(2)}) collective-permute-start(bf16[8,4,64,512]{3,2,0,1:T(8,128)(2,1)S(1)} %fusion.16), channel_id=1, source_target_pairs={{0,4},{4,0},{1,5},{5,1},{2,6},{6,2},{3,7},{7,3},{8,12},{12,8},{9,1... | collective-permute-start | bytes 6291464 | tf_op jit(solution)/shard_map/ppermute | solution.py:23
  60.0 11.2 %collective-permute-done.13 = f32[128,1024]{1,0:T(8,128)S(1)} collective-permute-done((f32[128,1024]{1,0:T(8,128)S(1)}, f32[128,1024]{1,0:T(8,128)S(1)}, u32[]{:S(2)}, u32[]{:S(2)}) %collective-permute-start.13) | collective-permute-done | bytes 524320 | tf_op jit(solution)/shard_map/ppermute | solution.py:64
  71.7 13.2 %collective-permute-done.14 = f32[128,1024]{1,0:T(8,128)S(1)} collective-permute-done((f32[128,1024]{1,0:T(8,128)S(1)}, f32[128,1024]{1,0:T(8,128)S(1)}, u32[]{:S(2)}, u32[]{:S(2)}) %collective-permute-start.14) | collective-permute-done | bytes 524320 | tf_op jit(solution)/shard_map/ppermute | solution.py:64
  112.1 16.9 %collective-permute-done.24 = bf16[4,128,1024]{2,1,0:T(8,128)(2,1)S(1)} collective-permute-done((bf16[4,128,1024]{2,1,0:T(8,128)(2,1)S(1)}, bf16[4,128,1024]{2,1,0:T(8,128)(2,1)S(1)}, u32[]{:S(2)}, u32[]{:S(2)}) %collective-permute-start.24) | collective-permute-done | bytes 1048608 | tf_op jit(solution)/shard_map/ppermute | solution.py:35
  137.1 13.5 %collective-permute-done.26 = bf16[4,128,1024]{2,1,0:T(8,128)(2,1)S(1)} collective-permute-done((bf16[4,128,1024]{2,1,0:T(8,128)(2,1)S(1)}, bf16[4,128,1024]{2,1,0:T(8,128)(2,1)S(1)}, u32[]{:S(2)}, u32[]{:S(2)}) %collective-permute-start.26) | collective-permute-done | bytes 1048608 | tf_op jit(solution)/shard_map/ppermute | solution.py:35
  157.5 14.7 %collective-permute-done.28 = bf16[4,128,1024]{2,1,0:T(8,128)(2,1)S(1)} collective-permute-done((bf16[4,128,1024]{2,1,0:T(8,128)(2,1)S(1)}, bf16[4,128,1024]{2,1,0:T(8,128)(2,1)S(1)}, u32[]{:S(2)}, u32[]{:S(2)}) %collective-permute-start.28) | collective-permute-done | bytes 1048608 | tf_op jit(solution)/shard_map/ppermute | solution.py:35
  177.3 8.7 %collective-permute-done.30 = bf16[2,128,1024]{2,1,0:T(8,128)(2,1)S(1)} collective-permute-done((bf16[2,128,1024]{2,1,0:T(8,128)(2,1)S(1)}, bf16[2,128,1024]{2,1,0:T(8,128)(2,1)S(1)}, u32[]{:S(2)}, u32[]{:S(2)}) %collective-permute-start.30) | collective-permute-done | bytes 524320 | tf_op jit(solution)/shard_map/ppermute | solution.py:31
  187.1 11.2 %collective-permute-start.32 = (bf16[8,4,128,1024]{3,2,1,0:T(8,128)(2,1)}, bf16[8,4,128,1024]{3,2,1,0:T(8,128)(2,1)}, u32[]{:S(2)}, u32[]{:S(2)}) collective-permute-start(bf16[8,4,128,1024]{3,2,1,0:T(8,128)(2,1)} %fusion), channel_id=1, source_target_pairs={{0,4},{4,0},{1,5},{5,1},{2,6},{6,2},{3,7},{7,3},{8,12},{12,8},{9,1... | collective-permute-start | bytes 25165832 | tf_op jit(solution)/shard_map/ppermute | solution.py:23
  225.8 5.7 %collective-permute-start.49 = (s32[8,4,64,31]{2,1,0,3:T(4,128)S(1)}, s32[8,4,64,31]{2,1,0,3:T(4,128)}, u32[]{:S(2)}, u32[]{:S(2)}) collective-permute-start(s32[8,4,64,31]{2,1,0,3:T(4,128)S(1)} %fusion.23), channel_id=1, source_target_pairs={{0,4},{4,0},{1,5},{5,1},{2,6},{6,2},{3,7},{7,3},{8,12},{12,8},{9,1... | collective-permute-start | bytes 761864 | tf_op jit(solution)/shard_map/ppermute | solution.py:23
  232.7 6.1 %broadcast_in_dim.382 = bf16[2,8,4,128,1024]{4,3,2,1,0:T(8,128)(2,1)} broadcast(bf16[]{:T(256)} %constant.594.clone.1), dimensions={} | broadcast | bytes 16777218 | tf_op jit(solution)/shard_map/broadcast_in_dim | solution.py:20
  238.7 8.3 %bitcast_dynamic-update-slice_fusion.1 = bf16[2,8,4,128,1024]{4,3,2,1,0:T(8,128)(2,1)} fusion(bf16[2,8,4,128,1024]{4,3,2,1,0:T(8,128)(2,1)} %broadcast_in_dim.382, s32[]{:T(128)S(6)} %select_n.438, bf16[8,4,128,1024]{3,2,1,0:T(8,128)(2,1)} %fusion), kind=kLoop, calls=%fused_computation.5 | loop fusion | bytes 16777220 | tf_op jit(solution)/shard_map/jit(dynamic_update_index_in_dim)/dynamic_update_slice | solution.py:21
  247.0 8.3 %bitcast_dynamic-update-slice_fusion = bf16[2,8,4,128,1024]{4,3,2,1,0:T(8,128)(2,1)} fusion(bf16[2,8,4,128,1024]{4,3,2,1,0:T(8,128)(2,1)} %bitcast_dynamic-update-slice_fusion.1, s32[]{:T(128)S(6)} %select_n.439, bf16[8,4,128,1024]{3,2,1,0:T(8,128)(2,1)} %collective-permute-done.32), kind=kLoop, calls=%fused_computation.4 | loop fusion | bytes 16777220 | tf_op jit(solution)/shard_map/jit(dynamic_update_index_in_dim)/dynamic_update_slice | solution.py:23
  255.4 9.8 %fusion.42 = (bf16[64,1,64,1024]{3,2,1,0:T(8,128)(2,1)S(1)}, bf16[64,1,64,1024]{3,2,1,0:T(8,128)(2,1)}) fusion(bf16[64,2,64,1024]{3,2,1,0:T(8,128)(2,1)} %bitcast.307), kind=kLoop, calls=%fused_computation.168 | loop fusion | bytes 33554432 | tf_op jit(solution)/shard_map/slice | solution.py:124
  271.2 15.4 %gather_fusion = f32[1984]{0:T(1024)S(1)} fusion(f32[64,4096]{1,0:T(8,128)S(1)} %fusion.20, s32[1984]{0:T(1024)S(1)} %reshape.81), kind=kCustom, calls=%fused_computation | custom fusion | bytes 31744 | tf_op jit(solution)/shard_map/jit(take_along_axis)/gather | solution.py:129
  300.1 6.4 %select_reduce_fusion.1 = f32[64,4096]{1,0:T(8,128)S(1)} fusion(f32[31,64]{1,0:T(8,128)S(1)} %copy.215, s32[31,64]{1,0:T(8,128)} %copy.214), kind=kLoop, calls=%fused_computation.2 | loop fusion | flops 24117248 | bytes 1064448 | tf_op jit(solution)/shard_map/reduce_sum | solution.py:141
  309.8 5.5 %fusion.1 = f32[128,1024]{1,0:T(8,128)} fusion(bf16[4096,1024]{1,0:T(8,128)(2,1)} %bitcast.311, bf16[64,4096]{1,0:T(8,128)(2,1)S(1)} %get-tuple-element.5, bf16[64,4096]{1,0:T(8,128)(2,1)S(1)} %get-tuple-element.6), kind=kOutput, calls=%fused_computation.13 | convolution fusion | flops 1075838976 | bytes 9961472 | tf_op jit(solution)/shard_map/dot_general | solution.py:85
  334.5 7.1 %collective-permute-start.62 = (f32[8,4,64,31]{2,1,0,3:T(4,128)S(1)}, f32[8,4,64,31]{2,1,0,3:T(4,128)S(1)}, u32[]{:S(2)}, u32[]{:S(2)}) collective-permute-start(f32[8,4,64,31]{2,1,0,3:T(4,128)S(1)} %fusion.24), channel_id=1, source_target_pairs={{0,4},{4,0},{1,5},{5,1},{2,6},{6,2},{3,7},{7,3},{8,12},{12,8},{9,1... | collective-permute-start | bytes 761864 | tf_op jit(solution)/shard_map/ppermute | solution.py:23
  348.1 4.8 fusion.5
  383.9 5.3 %collective-permute-start.71 = (f32[4,8,64,512]{3,2,1,0:T(8,128)}, f32[4,8,64,512]{3,2,1,0:T(8,128)}, u32[]{:S(2)}, u32[]{:S(2)}) collective-permute-start(f32[4,8,64,512]{3,2,1,0:T(8,128)} %dynamic-slice_bitcast_fusion), channel_id=1, source_target_pairs={{0,4},{4,0},{1,5},{5,1},{2,6},{6,2},{3,7},{7,3},{8,12},{12,8},{9,1... | collective-permute-start | bytes 12582920 | tf_op jit(solution)/shard_map/ppermute | solution.py:59
  389.1 7.1 %collective-permute-done.71 = f32[4,8,64,512]{3,2,1,0:T(8,128)} collective-permute-done((f32[4,8,64,512]{3,2,1,0:T(8,128)}, f32[4,8,64,512]{3,2,1,0:T(8,128)}, u32[]{:S(2)}, u32[]{:S(2)}) %collective-permute-start.71) | collective-permute-done | bytes 4194336 | tf_op jit(solution)/shard_map/ppermute | solution.py:59
  404.1 11.8 %collective-permute-done.72 = f32[4,64,512]{2,1,0:T(8,128)S(1)} collective-permute-done((f32[4,64,512]{2,1,0:T(8,128)S(1)}, f32[4,64,512]{2,1,0:T(8,128)S(1)}, u32[]{:S(2)}, u32[]{:S(2)}) %collective-permute-start.72) | collective-permute-done | bytes 524320 | tf_op jit(solution)/shard_map/ppermute | solution.py:64
  416.1 13.7 %collective-permute-done.73 = f32[4,64,512]{2,1,0:T(8,128)S(1)} collective-permute-done((f32[4,64,512]{2,1,0:T(8,128)S(1)}, f32[4,64,512]{2,1,0:T(8,128)S(1)}, u32[]{:S(2)}, u32[]{:S(2)}) %collective-permute-start.73) | collective-permute-done | bytes 524320 | tf_op jit(solution)/shard_map/ppermute | solution.py:64
  432.8 10.2 %collective-permute-done.74 = f32[4,64,512]{2,1,0:T(8,128)S(1)} collective-permute-done((f32[4,64,512]{2,1,0:T(8,128)S(1)}, f32[4,64,512]{2,1,0:T(8,128)S(1)}, u32[]{:S(2)}, u32[]{:S(2)}) %collective-permute-start.74) | collective-permute-done | bytes 524320 | tf_op jit(solution)/shard_map/ppermute | solution.py:64
  471.5 9.0 %collective-permute-start.94 = (f32[8,4,1024]{2,0,1:T(8,128)S(1)}, f32[8,4,1024]{2,0,1:T(8,128)S(1)}, u32[]{:S(2)}, u32[]{:S(2)}) collective-permute-start(f32[8,4,1024]{2,0,1:T(8,128)S(1)} %dynamic_update_slice.358), channel_id=1, source_target_pairs={{0,4},{4,0},{1,5},{5,1},{2,6},{6,2},{3,7},{7,3},{8,12},{12,8},{9,1... | collective-permute-start | bytes 393224 | tf_op jit(solution)/shard_map/ppermute | solution.py:23
  (401 shorter events, 261.9 us)
Async XLA Ops:
  39.9 11.3 %collective-permute-start.12 = (bf16[8,4,64,512]{3,2,0,1:T(8,128)(2,1)S(1)}, bf16[8,4,64,512]{3,2,0,1:T(8,128)(2,1)}, u32[]{:S(2)}, u32[]{:S(2)}) collective-permute-start(bf16[8,4,64,512]{3,2,0,1:T(8,128)(2,1)S(1)} %fusion.16), channel_id=1, source_target_pairs={{0,4},{4,0},{1,5},{5,1},{2,6},{6,2},{3,7},{7,3},{8,12},{12,8},{9,1... | collective-permute-start | bytes 6291464 | tf_op jit(solution)/shard_map/ppermute | solution.py:23
  56.7 14.5 %collective-permute-start.13 = (f32[128,1024]{1,0:T(8,128)S(1)}, f32[128,1024]{1,0:T(8,128)S(1)}, u32[]{:S(2)}, u32[]{:S(2)}) collective-permute-start(f32[128,1024]{1,0:T(8,128)S(1)} %bitcast.320), channel_id=1, source_target_pairs={{0,1},{1,2},{2,3},{3,0},{4,5},{5,6},{6,7},{7,4},{8,9},{9,10},{10,1... | collective-permute-start | bytes 1572872 | tf_op jit(solution)/shard_map/ppermute | solution.py:64
  58.5 13.2 %collective-permute-start.15 = (f32[128,1024]{1,0:T(8,128)S(1)}, f32[128,1024]{1,0:T(8,128)}, u32[]{:S(2)}, u32[]{:S(2)}) collective-permute-start(f32[128,1024]{1,0:T(8,128)S(1)} %bitcast.319), channel_id=1, source_target_pairs={{0,3},{1,0},{2,1},{3,2},{4,7},{5,4},{6,5},{7,6},{8,11},{9,8},{10,9... | collective-permute-start | bytes 1572872 | tf_op jit(solution)/shard_map/ppermute | solution.py:70
  71.3 13.6 %collective-permute-start.14 = (f32[128,1024]{1,0:T(8,128)S(1)}, f32[128,1024]{1,0:T(8,128)S(1)}, u32[]{:S(2)}, u32[]{:S(2)}) collective-permute-start(f32[128,1024]{1,0:T(8,128)S(1)} %bitcast_add_fusion.8), channel_id=1, source_target_pairs={{0,1},{1,2},{2,3},{3,0},{4,5},{5,6},{6,7},{7,4},{8,9},{9,10},{10,1... | collective-permute-start | bytes 1572872 | tf_op jit(solution)/shard_map/ppermute | solution.py:64
  108.4 20.6 %collective-permute-start.24 = (bf16[4,128,1024]{2,1,0:T(8,128)(2,1)S(1)}, bf16[4,128,1024]{2,1,0:T(8,128)(2,1)S(1)}, u32[]{:S(2)}, u32[]{:S(2)}) collective-permute-start(bf16[4,128,1024]{2,1,0:T(8,128)(2,1)S(1)} %fusion.17), channel_id=1, source_target_pairs={{0,8},{8,16},{16,24},{24,32},{32,40},{40,48},{48,56},{56,0},{1,9},... | collective-permute-start | bytes 3145736 | tf_op jit(solution)/shard_map/ppermute | solution.py:35
  109.0 19.9 %collective-permute-start.25 = (bf16[4,128,1024]{2,1,0:T(8,128)(2,1)S(1)}, bf16[4,128,1024]{2,1,0:T(8,128)(2,1)S(1)}, u32[]{:S(2)}, u32[]{:S(2)}) collective-permute-start(bf16[4,128,1024]{2,1,0:T(8,128)(2,1)S(1)} %fusion.17), channel_id=1, source_target_pairs={{0,56},{8,0},{16,8},{24,16},{32,24},{40,32},{48,40},{56,48},{1,57}... | collective-permute-start | bytes 3145736 | tf_op jit(solution)/shard_map/ppermute | solution.py:37
  129.0 21.6 %collective-permute-start.26 = (bf16[4,128,1024]{2,1,0:T(8,128)(2,1)S(1)}, bf16[4,128,1024]{2,1,0:T(8,128)(2,1)S(1)}, u32[]{:S(2)}, u32[]{:S(2)}) collective-permute-start(bf16[4,128,1024]{2,1,0:T(8,128)(2,1)S(1)} %collective-permute-done.24), channel_id=1, source_target_pairs={{0,8},{8,16},{16,24},{24,32},{32,40},{40,48},{48,56},{56,0},{1,9},... | collective-permute-start | bytes 3145736 | tf_op jit(solution)/shard_map/ppermute | solution.py:35
  129.0 21.6 %collective-permute-start.27 = (bf16[4,128,1024]{2,1,0:T(8,128)(2,1)S(1)}, bf16[4,128,1024]{2,1,0:T(8,128)(2,1)S(1)}, u32[]{:S(2)}, u32[]{:S(2)}) collective-permute-start(bf16[4,128,1024]{2,1,0:T(8,128)(2,1)S(1)} %collective-permute-done.25), channel_id=1, source_target_pairs={{0,56},{8,0},{16,8},{24,16},{32,24},{40,32},{48,40},{56,48},{1,57}... | collective-permute-start | bytes 3145736 | tf_op jit(solution)/shard_map/ppermute | solution.py:37
  150.6 21.6 %collective-permute-start.28 = (bf16[4,128,1024]{2,1,0:T(8,128)(2,1)S(1)}, bf16[4,128,1024]{2,1,0:T(8,128)(2,1)S(1)}, u32[]{:S(2)}, u32[]{:S(2)}) collective-permute-start(bf16[4,128,1024]{2,1,0:T(8,128)(2,1)S(1)} %collective-permute-done.26), channel_id=1, source_target_pairs={{0,8},{8,16},{16,24},{24,32},{32,40},{40,48},{48,56},{56,0},{1,9},... | collective-permute-start | bytes 3145736 | tf_op jit(solution)/shard_map/ppermute | solution.py:35
  150.6 21.7 %collective-permute-start.29 = (bf16[4,128,1024]{2,1,0:T(8,128)(2,1)S(1)}, bf16[4,128,1024]{2,1,0:T(8,128)(2,1)S(1)}, u32[]{:S(2)}, u32[]{:S(2)}) collective-permute-start(bf16[4,128,1024]{2,1,0:T(8,128)(2,1)S(1)} %collective-permute-done.27), channel_id=1, source_target_pairs={{0,56},{8,0},{16,8},{24,16},{32,24},{40,32},{48,40},{56,48},{1,57}... | collective-permute-start | bytes 3145736 | tf_op jit(solution)/shard_map/ppermute | solution.py:37
  172.2 13.7 %collective-permute-start.30 = (bf16[2,128,1024]{2,1,0:T(8,128)(2,1)S(1)}, bf16[2,128,1024]{2,1,0:T(8,128)(2,1)S(1)}, u32[]{:S(2)}, u32[]{:S(2)}) collective-permute-start(bf16[2,128,1024]{2,1,0:T(8,128)(2,1)S(1)} %slice.164), channel_id=1, source_target_pairs={{0,8},{8,16},{16,24},{24,32},{32,40},{40,48},{48,56},{56,0},{1,9},... | collective-permute-start | bytes 1572872 | tf_op jit(solution)/shard_map/ppermute | solution.py:31
  172.4 13.6 %collective-permute-start.31 = (bf16[2,128,1024]{2,1,0:T(8,128)(2,1)S(1)}, bf16[2,128,1024]{2,1,0:T(8,128)(2,1)S(1)}, u32[]{:S(2)}, u32[]{:S(2)}) collective-permute-start(bf16[2,128,1024]{2,1,0:T(8,128)(2,1)S(1)} %slice.165), channel_id=1, source_target_pairs={{0,56},{8,0},{16,8},{24,16},{32,24},{40,32},{48,40},{56,48},{1,57}... | collective-permute-start | bytes 1572872 | tf_op jit(solution)/shard_map/ppermute | solution.py:31
  187.1 60.0 %collective-permute-start.32 = (bf16[8,4,128,1024]{3,2,1,0:T(8,128)(2,1)}, bf16[8,4,128,1024]{3,2,1,0:T(8,128)(2,1)}, u32[]{:S(2)}, u32[]{:S(2)}) collective-permute-start(bf16[8,4,128,1024]{3,2,1,0:T(8,128)(2,1)} %fusion), channel_id=1, source_target_pairs={{0,4},{4,0},{1,5},{5,1},{2,6},{6,2},{3,7},{7,3},{8,12},{12,8},{9,1... | collective-permute-start | bytes 25165832 | tf_op jit(solution)/shard_map/ppermute | solution.py:23
  225.8 64.7 %collective-permute-start.49 = (s32[8,4,64,31]{2,1,0,3:T(4,128)S(1)}, s32[8,4,64,31]{2,1,0,3:T(4,128)}, u32[]{:S(2)}, u32[]{:S(2)}) collective-permute-start(s32[8,4,64,31]{2,1,0,3:T(4,128)S(1)} %fusion.23), channel_id=1, source_target_pairs={{0,4},{4,0},{1,5},{5,1},{2,6},{6,2},{3,7},{7,3},{8,12},{12,8},{9,1... | collective-permute-start | bytes 761864 | tf_op jit(solution)/shard_map/ppermute | solution.py:23
  383.9 12.4 %collective-permute-start.71 = (f32[4,8,64,512]{3,2,1,0:T(8,128)}, f32[4,8,64,512]{3,2,1,0:T(8,128)}, u32[]{:S(2)}, u32[]{:S(2)}) collective-permute-start(f32[4,8,64,512]{3,2,1,0:T(8,128)} %dynamic-slice_bitcast_fusion), channel_id=1, source_target_pairs={{0,4},{4,0},{1,5},{5,1},{2,6},{6,2},{3,7},{7,3},{8,12},{12,8},{9,1... | collective-permute-start | bytes 12582920 | tf_op jit(solution)/shard_map/ppermute | solution.py:59
  400.8 15.1 %collective-permute-start.72 = (f32[4,64,512]{2,1,0:T(8,128)S(1)}, f32[4,64,512]{2,1,0:T(8,128)S(1)}, u32[]{:S(2)}, u32[]{:S(2)}) collective-permute-start(f32[4,64,512]{2,1,0:T(8,128)S(1)} %get-tuple-element.23), channel_id=1, source_target_pairs={{0,8},{8,16},{16,24},{24,32},{32,40},{40,48},{48,56},{56,0},{1,9},... | collective-permute-start | bytes 1572872 | tf_op jit(solution)/shard_map/ppermute | solution.py:64
  400.9 15.2 %collective-permute-start.76 = (f32[4,64,512]{2,1,0:T(8,128)S(1)}, f32[4,64,512]{2,1,0:T(8,128)S(1)}, u32[]{:S(2)}, u32[]{:S(2)}) collective-permute-start(f32[4,64,512]{2,1,0:T(8,128)S(1)} %get-tuple-element.24), channel_id=1, source_target_pairs={{0,56},{8,0},{16,8},{24,16},{32,24},{40,32},{48,40},{56,48},{1,57}... | collective-permute-start | bytes 1572872 | tf_op jit(solution)/shard_map/ppermute | solution.py:69
  416.0 13.8 %collective-permute-start.73 = (f32[4,64,512]{2,1,0:T(8,128)S(1)}, f32[4,64,512]{2,1,0:T(8,128)S(1)}, u32[]{:S(2)}, u32[]{:S(2)}) collective-permute-start(f32[4,64,512]{2,1,0:T(8,128)S(1)} %bitcast_add_fusion.6), channel_id=1, source_target_pairs={{0,8},{8,16},{16,24},{24,32},{32,40},{40,48},{48,56},{56,0},{1,9},... | collective-permute-start | bytes 1572872 | tf_op jit(solution)/shard_map/ppermute | solution.py:64
  430.0 13.0 %collective-permute-start.74 = (f32[4,64,512]{2,1,0:T(8,128)S(1)}, f32[4,64,512]{2,1,0:T(8,128)S(1)}, u32[]{:S(2)}, u32[]{:S(2)}) collective-permute-start(f32[4,64,512]{2,1,0:T(8,128)S(1)} %get-tuple-element.21), channel_id=1, source_target_pairs={{0,8},{8,16},{16,24},{24,32},{32,40},{40,48},{48,56},{56,0},{1,9},... | collective-permute-start | bytes 1572872 | tf_op jit(solution)/shard_map/ppermute | solution.py:64
  430.1 12.9 %collective-permute-start.77 = (f32[4,64,512]{2,1,0:T(8,128)S(1)}, f32[4,64,512]{2,1,0:T(8,128)S(1)}, u32[]{:S(2)}, u32[]{:S(2)}) collective-permute-start(f32[4,64,512]{2,1,0:T(8,128)S(1)} %get-tuple-element.22), channel_id=1, source_target_pairs={{0,56},{8,0},{16,8},{24,16},{32,24},{40,32},{48,40},{56,48},{1,57}... | collective-permute-start | bytes 1572872 | tf_op jit(solution)/shard_map/ppermute | solution.py:69
  444.2 36.4 %collective-permute-start.75 = (f32[4,64,512]{2,1,0:T(8,128)}, f32[4,64,512]{2,1,0:T(8,128)S(1)}, u32[]{:S(2)}, u32[]{:S(2)}) collective-permute-start(f32[4,64,512]{2,1,0:T(8,128)} %get-tuple-element.19), channel_id=1, source_target_pairs={{0,8},{8,16},{16,24},{24,32},{32,40},{40,48},{48,56},{56,0},{1,9},... | collective-permute-start | bytes 1572872 | tf_op jit(solution)/shard_map/ppermute | solution.py:64
  444.2 36.4 %collective-permute-start.78 = (f32[4,64,512]{2,1,0:T(8,128)}, f32[4,64,512]{2,1,0:T(8,128)}, u32[]{:S(2)}, u32[]{:S(2)}) collective-permute-start(f32[4,64,512]{2,1,0:T(8,128)} %get-tuple-element.20), channel_id=1, source_target_pairs={{0,56},{8,0},{16,8},{24,16},{32,24},{40,32},{48,40},{56,48},{1,57}... | collective-permute-start | bytes 1572872 | tf_op jit(solution)/shard_map/ppermute | solution.py:70
  471.5 10.6 %collective-permute-start.94 = (f32[8,4,1024]{2,0,1:T(8,128)S(1)}, f32[8,4,1024]{2,0,1:T(8,128)S(1)}, u32[]{:S(2)}, u32[]{:S(2)}) collective-permute-start(f32[8,4,1024]{2,0,1:T(8,128)S(1)} %dynamic_update_slice.358), channel_id=1, source_target_pairs={{0,4},{4,0},{1,5},{5,1},{2,6},{6,2},{3,7},{7,3},{8,12},{12,8},{9,1... | collective-permute-start | bytes 393224 | tf_op jit(solution)/shard_map/ppermute | solution.py:23
  482.7 9.8 %collective-permute-start.81 = (f32[64,512]{1,0:T(8,128)S(1)}, f32[64,512]{1,0:T(8,128)S(1)}, u32[]{:S(2)}, u32[]{:S(2)}) collective-permute-start(f32[64,512]{1,0:T(8,128)S(1)} %get-tuple-element.30), channel_id=1, source_target_pairs={{0,192},{64,0},{128,64},{192,128},{1,193},{65,1},{129,65},{193,129... | collective-permute-start | bytes 393224 | tf_op jit(solution)/shard_map/ppermute | solution.py:70
  (84 other events, 749.6 us)

commit v4 on v3

--- a/solution.py
+++ b/solution.py
@@ -25,6 +25,10 @@
     n_bwd = (n - 1) // 2
     left = right = v
     for step in range(1, n_fwd + 1):
+        if step > n_bwd and v.size * v.dtype.itemsize < (1 << 19):
+            left = lax.ppermute(left, name, fwd)
+            out = lax.dynamic_update_index_in_dim(out, left, (me - step) % n, 0)
+            break
         if step > n_bwd:
             half = v.shape[0] // 2
             got = jnp.concatenate(
@@ -101,7 +105,6 @@
     owner_c = neg_owner % n_c
     pos = ((owner_c * n_z + owner_z) * n_x + owner_x) * pairs_here + neg_local
     pos_t = pos.T
-    pos_all_t = gather_dp(pos).reshape(total, -1).T
 
     weight_full = gather_dp(w_out).transpose(2, 1, 0, 3, 4).reshape(-1, heads)
     rows_a = attn.reshape(2 * pairs_here, heads)
@@ -135,7 +138,11 @@
     first = (jnp.arange(scores.shape[1]) == 0).astype(jnp.float32)[None, :]
     wts = LOSS_SCALE * (prob - first) / TAU
     wts_neg_t = wts[:, 1:].T
-    wts_all_t = gather_dp(wts[:, 1:]).reshape(total, -1).T
+    neg_count = pos.shape[1]
+    packed = jnp.concatenate([wts[:, 1:], pos.astype(jnp.float32)], axis=1)
+    packed_all_t = gather_dp(packed).reshape(total, -1).T
+    wts_all_t = packed_all_t[:neg_count]
+    pos_all_t = packed_all_t[neg_count:].astype(jnp.int32)
 
     cols = lax.broadcasted_iota(jnp.int32, (1, 1, total), 2)
     coef_q = jnp.sum(jnp.where(pos_t[:, :, None] == cols, wts_neg_t[:, :, None], 0.0), axis=0)

time: 504 us -> 470 us (0.933)
  starting transfers between devices: 172 us -> 118 us
  waiting for transfers between devices: 190 us -> 215 us
    ppermute x24 -> x31, waiting for transfers between devices: 79.6 us -> 132 us  [ring_collect(): left = lax.ppermute(left, name, fwd)]
    ppermute x14 -> x1, starting transfers between devices: 37.8 us -> 2.73 us  [ring_collect(): lax.ppermute(right[half:], name, bwd)]
    ppermute x14 -> x1, waiting for transfers between devices: 28.9 us -> 8.89 us  [ring_collect(): lax.ppermute(left[:half], name, fwd)]
    ppermute x24 -> x20, starting transfers between devices: 61.9 us -> 55 us  [ring_collect(): right = lax.ppermute(right, name, bwd)]
    ppermute x5 -> x4, starting transfers between devices: 40.4 us -> 35.3 us  [ring_collect(): lax.ppermute(v, name, fwd)]
    broadcast_in_dim x15 -> x12, local copies, waits for them, and re-layouts: 11.9 us -> 13.3 us  [ring_collect(): out = jnp.zeros((n,) + v.shape, v.dtype)]
    dynamic_update_slice x16 -> x13, local copies, waits for them, and re-layouts: 11.2 us -> 12.1 us  [ring_collect(): out = lax.dynamic_update_index_in_dim(out, v, me, 0)]
    dynamic_update_slice x5 -> x4, local copies, waits for them, and re-layouts: 11.4 us -> 11.3 us  [ring_collect(): lax.dynamic_update_index_in_dim(out, lax.ppermute(v, name, fwd), 1 - me, 0)]
  transfers between devices with their start and end apart: 95 -> 71, of which waited for: 48 -> 43; matrix products, arithmetic and copies ran while one was open for 19% -> 11% of each run, Pallas kernels for 0% -> 0%
where the time goes in v4:
time: 470 us; the launch traced here: 461 us
  waiting for transfers between devices  215 us (46%)
  starting transfers between devices  118 us (25%)
  local copies, waits for them, and re-layouts  85.5 us (18%)
  other arithmetic  22.4 us (5%)
  matrix products  18.1 us (4%)
    ppermute x31, waiting for transfers between devices, ring_collect(): left = lax.ppermute(left, name, fwd)  132 us
    ppermute x8, waiting for transfers between devices, ring_reduce(): acc_f = lax.ppermute(acc_f, name, fwd) + block(me + n_fwd - step)  63.6 us
    ppermute x20, starting transfers between devices, ring_collect(): right = lax.ppermute(right, name, bwd)  55 us
    ppermute x4, starting transfers between devices, ring_collect(): lax.ppermute(v, name, fwd)  35.3 us
    gather x3, local copies, waits for them, and re-layouts, shards(): neg_part = jnp.take_along_axis(all_scores, pos, axis=1)  15.7 us
    broadcast_in_dim x12, local copies, waits for them, and re-layouts, ring_collect(): out = jnp.zeros((n,) + v.shape, v.dtype)  13.3 us
    dot_general x3, matrix products, mm(): return jnp.dot(a, b, preferred_element_type=jnp.float32)  12.9 us
    dynamic_update_slice x13, local copies, waits for them, and re-layouts, ring_collect(): out = lax.dynamic_update_index_in_dim(out, v, me, 0)  12.1 us
  transfers between devices with their start and end apart: 71, of which 43 were waited for; matrix products, arithmetic and copies ran while one was open for 11% of the time, Pallas kernels for 0%

profile of v4, /device:TPU:1, one launch (start us, length us, event | category | flops | bytes accessed | tf_op | source)
XLA Modules:
  0.0 460.9 jit_solution(12406475227642550190)
XLA Ops:
  33.5 8.3 %collective-permute-done.9 = bf16[4,64,512]{2,1,0:T(8,128)(2,1)S(1)} collective-permute-done((bf16[4,64,512]{2,1,0:T(8,128)(2,1)S(1)}, bf16[4,64,512]{2,1,0:T(8,128)(2,1)S(1)}, u32[]{:S(2)}, u32[]{:S(2)}) %collective-permute-start.9) | collective-permute-done | bytes 262176 | tf_op jit(solution)/shard_map/ppermute | solution.py:29
  41.7 7.4 %collective-permute-start.10 = (bf16[8,4,64,512]{3,2,0,1:T(8,128)(2,1)S(1)}, bf16[8,4,64,512]{3,2,0,1:T(8,128)(2,1)}, u32[]{:S(2)}, u32[]{:S(2)}) collective-permute-start(bf16[8,4,64,512]{3,2,0,1:T(8,128)(2,1)S(1)} %bitcast_dynamic-update-slice_fusion.28), channel_id=1, source_target_pairs={{0,4},{4,0},{1,5},{5,1},{2,6},{6,2},{3,7},{7,3},{8,12},{12,8},{9,1... | collective-permute-start | bytes 6291464 | tf_op jit(solution)/shard_map/ppermute | solution.py:23
  60.9 10.9 %collective-permute-done.11 = f32[128,1024]{1,0:T(8,128)S(1)} collective-permute-done((f32[128,1024]{1,0:T(8,128)S(1)}, f32[128,1024]{1,0:T(8,128)S(1)}, u32[]{:S(2)}, u32[]{:S(2)}) %collective-permute-start.11) | collective-permute-done | bytes 524320 | tf_op jit(solution)/shard_map/ppermute | solution.py:68
  72.4 13.1 %collective-permute-done.12 = f32[128,1024]{1,0:T(8,128)S(1)} collective-permute-done((f32[128,1024]{1,0:T(8,128)S(1)}, f32[128,1024]{1,0:T(8,128)S(1)}, u32[]{:S(2)}, u32[]{:S(2)}) %collective-permute-start.12) | collective-permute-done | bytes 524320 | tf_op jit(solution)/shard_map/ppermute | solution.py:68
  100.9 7.5 %collective-permute-done.19 = bf16[128,1024]{1,0:T(8,128)(2,1)S(1)} collective-permute-done((bf16[128,1024]{1,0:T(8,128)(2,1)S(1)}, bf16[128,1024]{1,0:T(8,128)(2,1)S(1)}, u32[]{:S(2)}, u32[]{:S(2)}) %collective-permute-start.19) | collective-permute-done | bytes 262176 | tf_op jit(solution)/shard_map/ppermute | solution.py:29
  111.2 16.6 %collective-permute-done.20 = bf16[4,128,1024]{2,1,0:T(8,128)(2,1)S(1)} collective-permute-done((bf16[4,128,1024]{2,1,0:T(8,128)(2,1)S(1)}, bf16[4,128,1024]{2,1,0:T(8,128)(2,1)S(1)}, u32[]{:S(2)}, u32[]{:S(2)}) %collective-permute-start.20) | collective-permute-done | bytes 1048608 | tf_op jit(solution)/shard_map/ppermute | solution.py:39
  135.9 13.6 %collective-permute-done.22 = bf16[4,128,1024]{2,1,0:T(8,128)(2,1)S(1)} collective-permute-done((bf16[4,128,1024]{2,1,0:T(8,128)(2,1)S(1)}, bf16[4,128,1024]{2,1,0:T(8,128)(2,1)S(1)}, u32[]{:S(2)}, u32[]{:S(2)}) %collective-permute-start.22) | collective-permute-done | bytes 1048608 | tf_op jit(solution)/shard_map/ppermute | solution.py:39
  156.4 14.7 %collective-permute-done.24 = bf16[4,128,1024]{2,1,0:T(8,128)(2,1)S(1)} collective-permute-done((bf16[4,128,1024]{2,1,0:T(8,128)(2,1)S(1)}, bf16[4,128,1024]{2,1,0:T(8,128)(2,1)S(1)}, u32[]{:S(2)}, u32[]{:S(2)}) %collective-permute-start.24) | collective-permute-done | bytes 1048608 | tf_op jit(solution)/shard_map/ppermute | solution.py:39
  176.3 8.9 %collective-permute-done.26 = bf16[2,128,1024]{2,1,0:T(8,128)(2,1)S(1)} collective-permute-done((bf16[2,128,1024]{2,1,0:T(8,128)(2,1)S(1)}, bf16[2,128,1024]{2,1,0:T(8,128)(2,1)S(1)}, u32[]{:S(2)}, u32[]{:S(2)}) %collective-permute-start.26) | collective-permute-done | bytes 524320 | tf_op jit(solution)/shard_map/ppermute | solution.py:35
  186.3 10.3 %collective-permute-start.28 = (bf16[8,4,128,1024]{3,2,1,0:T(8,128)(2,1)}, bf16[8,4,128,1024]{3,2,1,0:T(8,128)(2,1)}, u32[]{:S(2)}, u32[]{:S(2)}) collective-permute-start(bf16[8,4,128,1024]{3,2,1,0:T(8,128)(2,1)} %fusion), channel_id=1, source_target_pairs={{0,4},{4,0},{1,5},{5,1},{2,6},{6,2},{3,7},{7,3},{8,12},{12,8},{9,1... | collective-permute-start | bytes 25165832 | tf_op jit(solution)/shard_map/ppermute | solution.py:23
  197.3 6.1 %broadcast_in_dim.328 = bf16[2,8,4,128,1024]{4,3,2,1,0:T(8,128)(2,1)} broadcast(bf16[]{:T(256)} %constant.537.clone.1), dimensions={} | broadcast | bytes 16777218 | tf_op jit(solution)/shard_map/broadcast_in_dim | solution.py:20
  203.3 8.3 %bitcast_dynamic-update-slice_fusion.1 = bf16[2,8,4,128,1024]{4,3,2,1,0:T(8,128)(2,1)} fusion(bf16[2,8,4,128,1024]{4,3,2,1,0:T(8,128)(2,1)} %broadcast_in_dim.328, s32[]{:T(128)S(6)} %select_n.401, bf16[8,4,128,1024]{3,2,1,0:T(8,128)(2,1)} %fusion), kind=kLoop, calls=%fused_computation.5 | loop fusion | bytes 16777220 | tf_op jit(solution)/shard_map/jit(dynamic_update_index_in_dim)/dynamic_update_slice | solution.py:21
  211.6 8.3 %bitcast_dynamic-update-slice_fusion = bf16[2,8,4,128,1024]{4,3,2,1,0:T(8,128)(2,1)} fusion(bf16[2,8,4,128,1024]{4,3,2,1,0:T(8,128)(2,1)} %bitcast_dynamic-update-slice_fusion.1, s32[]{:T(128)S(6)} %select_n.402, bf16[8,4,128,1024]{3,2,1,0:T(8,128)(2,1)} %collective-permute-done.28), kind=kLoop, calls=%fused_computation.4 | loop fusion | bytes 16777220 | tf_op jit(solution)/shard_map/jit(dynamic_update_index_in_dim)/dynamic_update_slice | solution.py:23
  219.9 9.8 %fusion.35 = (bf16[64,1,64,1024]{3,2,1,0:T(8,128)(2,1)S(1)}, bf16[64,1,64,1024]{3,2,1,0:T(8,128)(2,1)}) fusion(bf16[64,2,64,1024]{3,2,1,0:T(8,128)(2,1)} %bitcast.244), kind=kLoop, calls=%fused_computation.146 | loop fusion | bytes 33554432 | tf_op jit(solution)/shard_map/slice | solution.py:127
  235.6 15.4 %gather_fusion = f32[1984]{0:T(1024)S(1)} fusion(f32[64,4096]{1,0:T(8,128)S(1)} %fusion.17, s32[1984]{0:T(1024)S(1)} %reshape.77), kind=kCustom, calls=%fused_computation | custom fusion | bytes 31744 | tf_op jit(solution)/shard_map/jit(take_along_axis)/gather | solution.py:132
  262.6 5.5 %select_reduce_fusion.1 = f32[64,4096]{1,0:T(8,128)S(1)} fusion(f32[31,64]{1,0:T(8,128)S(1)} %copy.105, s32[31,64]{1,0:T(8,128)S(1)} %copy.104), kind=kLoop, calls=%fused_computation.2 | loop fusion | flops 24117248 | bytes 1064448 | tf_op jit(solution)/shard_map/reduce_sum | solution.py:148
  290.3 5.1 %collective-permute-done.41 = f32[4,64,62]{1,0,2:T(4,128)S(1)} collective-permute-done((f32[4,64,62]{1,0,2:T(4,128)S(1)}, f32[4,64,62]{1,0,2:T(4,128)S(1)}, u32[]{:S(2)}, u32[]{:S(2)}) %collective-permute-start.41) | collective-permute-done | bytes 63520 | tf_op jit(solution)/shard_map/ppermute | solution.py:29
  295.4 7.8 %collective-permute-start.42 = (f32[8,4,64,62]{2,1,0,3:T(4,128)S(1)}, f32[8,4,64,62]{2,1,0,3:T(4,128)S(1)}, u32[]{:S(2)}, u32[]{:S(2)}) collective-permute-start(f32[8,4,64,62]{2,1,0,3:T(4,128)S(1)} %bitcast_dynamic-update-slice_fusion.38), channel_id=1, source_target_pairs={{0,4},{4,0},{1,5},{5,1},{2,6},{6,2},{3,7},{7,3},{8,12},{12,8},{9,1... | collective-permute-start | bytes 1523720 | tf_op jit(solution)/shard_map/ppermute | solution.py:23
  339.1 6.4 %collective-permute-done.48 = bf16[128,1024]{1,0:T(8,128)(2,1)S(1)} collective-permute-done((bf16[128,1024]{1,0:T(8,128)(2,1)S(1)}, bf16[128,1024]{1,0:T(8,128)(2,1)S(1)}, u32[]{:S(2)}, u32[]{:S(2)}) %collective-permute-start.48) | collective-permute-done | bytes 262176 | tf_op jit(solution)/shard_map/ppermute | solution.py:29
  356.2 7.1 %collective-permute-done.49 = f32[4,8,64,512]{3,2,1,0:T(8,128)} collective-permute-done((f32[4,8,64,512]{3,2,1,0:T(8,128)}, f32[4,8,64,512]{3,2,1,0:T(8,128)}, u32[]{:S(2)}, u32[]{:S(2)}) %collective-permute-start.49) | collective-permute-done | bytes 4194336 | tf_op jit(solution)/shard_map/ppermute | solution.py:63
  370.7 11.6 %collective-permute-done.50 = f32[4,64,512]{2,1,0:T(8,128)S(1)} collective-permute-done((f32[4,64,512]{2,1,0:T(8,128)S(1)}, f32[4,64,512]{2,1,0:T(8,128)S(1)}, u32[]{:S(2)}, u32[]{:S(2)}) %collective-permute-start.50) | collective-permute-done | bytes 524320 | tf_op jit(solution)/shard_map/ppermute | solution.py:68
  382.5 13.4 %collective-permute-done.51 = f32[4,64,512]{2,1,0:T(8,128)S(1)} collective-permute-done((f32[4,64,512]{2,1,0:T(8,128)S(1)}, f32[4,64,512]{2,1,0:T(8,128)S(1)}, u32[]{:S(2)}, u32[]{:S(2)}) %collective-permute-start.51) | collective-permute-done | bytes 524320 | tf_op jit(solution)/shard_map/ppermute | solution.py:68
  398.9 9.9 %collective-permute-done.52 = f32[4,64,512]{2,1,0:T(8,128)S(1)} collective-permute-done((f32[4,64,512]{2,1,0:T(8,128)S(1)}, f32[4,64,512]{2,1,0:T(8,128)S(1)}, u32[]{:S(2)}, u32[]{:S(2)}) %collective-permute-start.52) | collective-permute-done | bytes 524320 | tf_op jit(solution)/shard_map/ppermute | solution.py:68
  436.8 9.7 %collective-permute-start.70 = (f32[8,4,1024]{2,0,1:T(8,128)S(1)}, f32[8,4,1024]{2,0,1:T(8,128)S(1)}, u32[]{:S(2)}, u32[]{:S(2)}) collective-permute-start(f32[8,4,1024]{2,0,1:T(8,128)S(1)} %dynamic_update_slice.299), channel_id=1, source_target_pairs={{0,4},{4,0},{1,5},{5,1},{2,6},{6,2},{3,7},{7,3},{8,12},{12,8},{9,1... | collective-permute-start | bytes 393224 | tf_op jit(solution)/shard_map/ppermute | solution.py:23
  (297 shorter events, 223.0 us)
Async XLA Ops:
  10.2 9.6 %collective-permute-start.3 = (bf16[4,64,512]{2,1,0:T(8,128)(2,1)S(1)}, bf16[4,64,512]{2,1,0:T(8,128)(2,1)S(1)}, u32[]{:S(2)}, u32[]{:S(2)}) collective-permute-start(bf16[4,64,512]{2,1,0:T(8,128)(2,1)S(1)} %bitcast_dynamic-update-slice_fusion.39), channel_id=1, source_target_pairs={{0,8},{8,16},{16,24},{24,32},{32,40},{40,48},{48,56},{56,0},{1,9},... | collective-permute-start | bytes 786440 | tf_op jit(solution)/shard_map/ppermute | solution.py:39
  41.7 11.4 %collective-permute-start.10 = (bf16[8,4,64,512]{3,2,0,1:T(8,128)(2,1)S(1)}, bf16[8,4,64,512]{3,2,0,1:T(8,128)(2,1)}, u32[]{:S(2)}, u32[]{:S(2)}) collective-permute-start(bf16[8,4,64,512]{3,2,0,1:T(8,128)(2,1)S(1)} %bitcast_dynamic-update-slice_fusion.28), channel_id=1, source_target_pairs={{0,4},{4,0},{1,5},{5,1},{2,6},{6,2},{3,7},{7,3},{8,12},{12,8},{9,1... | collective-permute-start | bytes 6291464 | tf_op jit(solution)/shard_map/ppermute | solution.py:23
  57.3 14.5 %collective-permute-start.11 = (f32[128,1024]{1,0:T(8,128)S(1)}, f32[128,1024]{1,0:T(8,128)S(1)}, u32[]{:S(2)}, u32[]{:S(2)}) collective-permute-start(f32[128,1024]{1,0:T(8,128)S(1)} %bitcast.256), channel_id=1, source_target_pairs={{0,1},{1,2},{2,3},{3,0},{4,5},{5,6},{6,7},{7,4},{8,9},{9,10},{10,1... | collective-permute-start | bytes 1572872 | tf_op jit(solution)/shard_map/ppermute | solution.py:68
  59.1 13.4 %collective-permute-start.13 = (f32[128,1024]{1,0:T(8,128)S(1)}, f32[128,1024]{1,0:T(8,128)}, u32[]{:S(2)}, u32[]{:S(2)}) collective-permute-start(f32[128,1024]{1,0:T(8,128)S(1)} %bitcast.255), channel_id=1, source_target_pairs={{0,3},{1,0},{2,1},{3,2},{4,7},{5,4},{6,5},{7,6},{8,11},{9,8},{10,9... | collective-permute-start | bytes 1572872 | tf_op jit(solution)/shard_map/ppermute | solution.py:74
  71.9 13.6 %collective-permute-start.12 = (f32[128,1024]{1,0:T(8,128)S(1)}, f32[128,1024]{1,0:T(8,128)S(1)}, u32[]{:S(2)}, u32[]{:S(2)}) collective-permute-start(f32[128,1024]{1,0:T(8,128)S(1)} %bitcast_add_fusion.8), channel_id=1, source_target_pairs={{0,1},{1,2},{2,3},{3,0},{4,5},{5,6},{6,7},{7,4},{8,9},{9,10},{10,1... | collective-permute-start | bytes 1572872 | tf_op jit(solution)/shard_map/ppermute | solution.py:68
  108.5 19.4 %collective-permute-start.20 = (bf16[4,128,1024]{2,1,0:T(8,128)(2,1)S(1)}, bf16[4,128,1024]{2,1,0:T(8,128)(2,1)S(1)}, u32[]{:S(2)}, u32[]{:S(2)}) collective-permute-start(bf16[4,128,1024]{2,1,0:T(8,128)(2,1)S(1)} %bitcast_dynamic-update-slice_fusion.24), channel_id=1, source_target_pairs={{0,8},{8,16},{16,24},{24,32},{32,40},{40,48},{48,56},{56,0},{1,9},... | collective-permute-start | bytes 3145736 | tf_op jit(solution)/shard_map/ppermute | solution.py:39
  108.6 19.3 %collective-permute-start.21 = (bf16[4,128,1024]{2,1,0:T(8,128)(2,1)S(1)}, bf16[4,128,1024]{2,1,0:T(8,128)(2,1)S(1)}, u32[]{:S(2)}, u32[]{:S(2)}) collective-permute-start(bf16[4,128,1024]{2,1,0:T(8,128)(2,1)S(1)} %bitcast_dynamic-update-slice_fusion.24), channel_id=1, source_target_pairs={{0,56},{8,0},{16,8},{24,16},{32,24},{40,32},{48,40},{56,48},{1,57}... | collective-permute-start | bytes 3145736 | tf_op jit(solution)/shard_map/ppermute | solution.py:41
  127.9 21.6 %collective-permute-start.22 = (bf16[4,128,1024]{2,1,0:T(8,128)(2,1)S(1)}, bf16[4,128,1024]{2,1,0:T(8,128)(2,1)S(1)}, u32[]{:S(2)}, u32[]{:S(2)}) collective-permute-start(bf16[4,128,1024]{2,1,0:T(8,128)(2,1)S(1)} %collective-permute-done.20), channel_id=1, source_target_pairs={{0,8},{8,16},{16,24},{24,32},{32,40},{40,48},{48,56},{56,0},{1,9},... | collective-permute-start | bytes 3145736 | tf_op jit(solution)/shard_map/ppermute | solution.py:39
  127.9 21.6 %collective-permute-start.23 = (bf16[4,128,1024]{2,1,0:T(8,128)(2,1)S(1)}, bf16[4,128,1024]{2,1,0:T(8,128)(2,1)S(1)}, u32[]{:S(2)}, u32[]{:S(2)}) collective-permute-start(bf16[4,128,1024]{2,1,0:T(8,128)(2,1)S(1)} %collective-permute-done.21), channel_id=1, source_target_pairs={{0,56},{8,0},{16,8},{24,16},{32,24},{40,32},{48,40},{56,48},{1,57}... | collective-permute-start | bytes 3145736 | tf_op jit(solution)/shard_map/ppermute | solution.py:41
  149.5 21.6 %collective-permute-start.24 = (bf16[4,128,1024]{2,1,0:T(8,128)(2,1)S(1)}, bf16[4,128,1024]{2,1,0:T(8,128)(2,1)S(1)}, u32[]{:S(2)}, u32[]{:S(2)}) collective-permute-start(bf16[4,128,1024]{2,1,0:T(8,128)(2,1)S(1)} %collective-permute-done.22), channel_id=1, source_target_pairs={{0,8},{8,16},{16,24},{24,32},{32,40},{40,48},{48,56},{56,0},{1,9},... | collective-permute-start | bytes 3145736 | tf_op jit(solution)/shard_map/ppermute | solution.py:39
  149.5 21.9 %collective-permute-start.25 = (bf16[4,128,1024]{2,1,0:T(8,128)(2,1)S(1)}, bf16[4,128,1024]{2,1,0:T(8,128)(2,1)S(1)}, u32[]{:S(2)}, u32[]{:S(2)}) collective-permute-start(bf16[4,128,1024]{2,1,0:T(8,128)(2,1)S(1)} %collective-permute-done.23), channel_id=1, source_target_pairs={{0,56},{8,0},{16,8},{24,16},{32,24},{40,32},{48,40},{56,48},{1,57}... | collective-permute-start | bytes 3145736 | tf_op jit(solution)/shard_map/ppermute | solution.py:41
  171.1 14.1 %collective-permute-start.26 = (bf16[2,128,1024]{2,1,0:T(8,128)(2,1)S(1)}, bf16[2,128,1024]{2,1,0:T(8,128)(2,1)S(1)}, u32[]{:S(2)}, u32[]{:S(2)}) collective-permute-start(bf16[2,128,1024]{2,1,0:T(8,128)(2,1)S(1)} %slice.62), channel_id=1, source_target_pairs={{0,8},{8,16},{16,24},{24,32},{32,40},{40,48},{48,56},{56,0},{1,9},... | collective-permute-start | bytes 1572872 | tf_op jit(solution)/shard_map/ppermute | solution.py:35
  171.5 13.8 %collective-permute-start.27 = (bf16[2,128,1024]{2,1,0:T(8,128)(2,1)S(1)}, bf16[2,128,1024]{2,1,0:T(8,128)(2,1)S(1)}, u32[]{:S(2)}, u32[]{:S(2)}) collective-permute-start(bf16[2,128,1024]{2,1,0:T(8,128)(2,1)S(1)} %slice.63), channel_id=1, source_target_pairs={{0,56},{8,0},{16,8},{24,16},{32,24},{40,32},{48,40},{56,48},{1,57}... | collective-permute-start | bytes 1572872 | tf_op jit(solution)/shard_map/ppermute | solution.py:35
  186.3 25.3 %collective-permute-start.28 = (bf16[8,4,128,1024]{3,2,1,0:T(8,128)(2,1)}, bf16[8,4,128,1024]{3,2,1,0:T(8,128)(2,1)}, u32[]{:S(2)}, u32[]{:S(2)}) collective-permute-start(bf16[8,4,128,1024]{3,2,1,0:T(8,128)(2,1)} %fusion), channel_id=1, source_target_pairs={{0,4},{4,0},{1,5},{5,1},{2,6},{6,2},{3,7},{7,3},{8,12},{12,8},{9,1... | collective-permute-start | bytes 25165832 | tf_op jit(solution)/shard_map/ppermute | solution.py:23
  295.4 15.6 %collective-permute-start.42 = (f32[8,4,64,62]{2,1,0,3:T(4,128)S(1)}, f32[8,4,64,62]{2,1,0,3:T(4,128)S(1)}, u32[]{:S(2)}, u32[]{:S(2)}) collective-permute-start(f32[8,4,64,62]{2,1,0,3:T(4,128)S(1)} %bitcast_dynamic-update-slice_fusion.38), channel_id=1, source_target_pairs={{0,4},{4,0},{1,5},{5,1},{2,6},{6,2},{3,7},{7,3},{8,12},{12,8},{9,1... | collective-permute-start | bytes 1523720 | tf_op jit(solution)/shard_map/ppermute | solution.py:23
  351.9 11.4 %collective-permute-start.49 = (f32[4,8,64,512]{3,2,1,0:T(8,128)}, f32[4,8,64,512]{3,2,1,0:T(8,128)}, u32[]{:S(2)}, u32[]{:S(2)}) collective-permute-start(f32[4,8,64,512]{3,2,1,0:T(8,128)} %dynamic-slice_bitcast_fusion), channel_id=1, source_target_pairs={{0,4},{4,0},{1,5},{5,1},{2,6},{6,2},{3,7},{7,3},{8,12},{12,8},{9,1... | collective-permute-start | bytes 12582920 | tf_op jit(solution)/shard_map/ppermute | solution.py:63
  367.9 14.4 %collective-permute-start.50 = (f32[4,64,512]{2,1,0:T(8,128)S(1)}, f32[4,64,512]{2,1,0:T(8,128)S(1)}, u32[]{:S(2)}, u32[]{:S(2)}) collective-permute-start(f32[4,64,512]{2,1,0:T(8,128)S(1)} %get-tuple-element.23), channel_id=1, source_target_pairs={{0,8},{8,16},{16,24},{24,32},{32,40},{40,48},{48,56},{56,0},{1,9},... | collective-permute-start | bytes 1572872 | tf_op jit(solution)/shard_map/ppermute | solution.py:68
  368.0 14.5 %collective-permute-start.54 = (f32[4,64,512]{2,1,0:T(8,128)S(1)}, f32[4,64,512]{2,1,0:T(8,128)S(1)}, u32[]{:S(2)}, u32[]{:S(2)}) collective-permute-start(f32[4,64,512]{2,1,0:T(8,128)S(1)} %get-tuple-element.24), channel_id=1, source_target_pairs={{0,56},{8,0},{16,8},{24,16},{32,24},{40,32},{48,40},{56,48},{1,57}... | collective-permute-start | bytes 1572872 | tf_op jit(solution)/shard_map/ppermute | solution.py:73
  382.4 13.5 %collective-permute-start.51 = (f32[4,64,512]{2,1,0:T(8,128)S(1)}, f32[4,64,512]{2,1,0:T(8,128)S(1)}, u32[]{:S(2)}, u32[]{:S(2)}) collective-permute-start(f32[4,64,512]{2,1,0:T(8,128)S(1)} %bitcast_add_fusion.6), channel_id=1, source_target_pairs={{0,8},{8,16},{16,24},{24,32},{32,40},{40,48},{48,56},{56,0},{1,9},... | collective-permute-start | bytes 1572872 | tf_op jit(solution)/shard_map/ppermute | solution.py:68
  396.2 12.7 %collective-permute-start.52 = (f32[4,64,512]{2,1,0:T(8,128)S(1)}, f32[4,64,512]{2,1,0:T(8,128)S(1)}, u32[]{:S(2)}, u32[]{:S(2)}) collective-permute-start(f32[4,64,512]{2,1,0:T(8,128)S(1)} %get-tuple-element.21), channel_id=1, source_target_pairs={{0,8},{8,16},{16,24},{24,32},{32,40},{40,48},{48,56},{56,0},{1,9},... | collective-permute-start | bytes 1572872 | tf_op jit(solution)/shard_map/ppermute | solution.py:68
  396.3 12.6 %collective-permute-start.55 = (f32[4,64,512]{2,1,0:T(8,128)S(1)}, f32[4,64,512]{2,1,0:T(8,128)S(1)}, u32[]{:S(2)}, u32[]{:S(2)}) collective-permute-start(f32[4,64,512]{2,1,0:T(8,128)S(1)} %get-tuple-element.22), channel_id=1, source_target_pairs={{0,56},{8,0},{16,8},{24,16},{32,24},{40,32},{48,40},{56,48},{1,57}... | collective-permute-start | bytes 1572872 | tf_op jit(solution)/shard_map/ppermute | solution.py:73
  410.1 36.5 %collective-permute-start.53 = (f32[4,64,512]{2,1,0:T(8,128)}, f32[4,64,512]{2,1,0:T(8,128)S(1)}, u32[]{:S(2)}, u32[]{:S(2)}) collective-permute-start(f32[4,64,512]{2,1,0:T(8,128)} %get-tuple-element.19), channel_id=1, source_target_pairs={{0,8},{8,16},{16,24},{24,32},{32,40},{40,48},{48,56},{56,0},{1,9},... | collective-permute-start | bytes 1572872 | tf_op jit(solution)/shard_map/ppermute | solution.py:68
  410.1 36.5 %collective-permute-start.56 = (f32[4,64,512]{2,1,0:T(8,128)}, f32[4,64,512]{2,1,0:T(8,128)}, u32[]{:S(2)}, u32[]{:S(2)}) collective-permute-start(f32[4,64,512]{2,1,0:T(8,128)} %get-tuple-element.20), channel_id=1, source_target_pairs={{0,56},{8,0},{16,8},{24,16},{32,24},{40,32},{48,40},{56,48},{1,57}... | collective-permute-start | bytes 1572872 | tf_op jit(solution)/shard_map/ppermute | solution.py:74
  436.8 11.3 %collective-permute-start.70 = (f32[8,4,1024]{2,0,1:T(8,128)S(1)}, f32[8,4,1024]{2,0,1:T(8,128)S(1)}, u32[]{:S(2)}, u32[]{:S(2)}) collective-permute-start(f32[8,4,1024]{2,0,1:T(8,128)S(1)} %dynamic_update_slice.299), channel_id=1, source_target_pairs={{0,4},{4,0},{1,5},{5,1},{2,6},{6,2},{3,7},{7,3},{8,12},{12,8},{9,1... | collective-permute-start | bytes 393224 | tf_op jit(solution)/shard_map/ppermute | solution.py:23
  (56 other events, 499.4 us)

commit v5 on v4

--- a/solution.py
+++ b/solution.py
@@ -20,7 +20,8 @@
     out = jnp.zeros((n,) + v.shape, v.dtype)
     out = lax.dynamic_update_index_in_dim(out, v, me, 0)
     if n == 2:
-        return lax.dynamic_update_index_in_dim(out, lax.ppermute(v, name, fwd), 1 - me, 0)
+        pair = jnp.stack([v, lax.ppermute(v, name, fwd)])
+        return jnp.where(me == 0, pair, pair[::-1])
     n_fwd = n // 2
     n_bwd = (n - 1) // 2
     left = right = v
@@ -43,6 +44,39 @@
     return out
 
 
+def ring_blocks(v, name, n):
+    if n == 1:
+        return [v]
+    fwd = [(i, (i + 1) % n) for i in range(n)]
+    bwd = [(i, (i - 1) % n) for i in range(n)]
+    if n == 2:
+        return [v, lax.ppermute(v, name, fwd)]
+    n_fwd = n // 2
+    n_bwd = (n - 1) // 2
+    blocks = [None] * n
+    blocks[0] = v
+    left = right = v
+    for step in range(1, n_fwd + 1):
+        if step > n_bwd and v.size * v.dtype.itemsize >= (1 << 19):
+            half = v.shape[0] // 2
+            blocks[n - step] = jnp.concatenate(
+                [lax.ppermute(left[:half], name, fwd), lax.ppermute(right[half:], name, bwd)], axis=0
+            )
+            break
+        left = lax.ppermute(left, name, fwd)
+        blocks[n - step] = left
+        if step <= n_bwd:
+            right = lax.ppermute(right, name, bwd)
+            blocks[step] = right
+    return blocks
+
+
+def gather_rel(v):
+    gx = jnp.stack(ring_blocks(v, "x", lax.axis_size("x")))
+    gz = jnp.stack(ring_blocks(gx, "z", lax.axis_size("z")))
+    return ring_blocks(gz, "c", lax.axis_size("c"))
+
+
 def gather_dp(v):
     gx = ring_collect(v, "x", lax.axis_size("x"))
     gz = ring_collect(gx, "z", lax.axis_size("z"))
@@ -100,10 +134,10 @@
 
     n_x = lax.axis_size("x")
     n_z = lax.axis_size("z")
-    owner_x = neg_owner // (n_z * n_c)
-    owner_z = (neg_owner // n_c) % n_z
-    owner_c = neg_owner % n_c
-    pos = ((owner_c * n_z + owner_z) * n_x + owner_x) * pairs_here + neg_local
+    step_x = (neg_owner // (n_z * n_c) - lax.axis_index("x")) % n_x
+    step_z = ((neg_owner // n_c) % n_z - lax.axis_index("z")) % n_z
+    step_c = (neg_owner % n_c - lax.axis_index("c")) % n_c
+    pos = ((step_c * n_z + step_z) * n_x + step_x) * pairs_here + neg_local
     pos_t = pos.T
 
     weight_full = gather_dp(w_out).transpose(2, 1, 0, 3, 4).reshape(-1, heads)
@@ -122,14 +156,15 @@
     docs = emb[pairs_here:]
     query_f = query.astype(jnp.float32)
     docs_f = docs.astype(jnp.float32)
-    emb_all = gather_dp(emb).reshape(n_xz * n_c, 2, pairs_here, feats)
-    q_all = emb_all[:, 0].reshape(total, feats)
-    e_all = emb_all[:, 1].reshape(total, feats)
+    emb_parts = [b.reshape(n_xz, 2, pairs_here, feats) for b in gather_rel(emb)]
+    q_all = jnp.stack([b[:, 0] for b in emb_parts]).reshape(total, feats)
+    e_all = jnp.stack([b[:, 1] for b in emb_parts]).reshape(total, feats)
 
     all_scores = lax.dot_general(
         query, e_all, (((1,), (1,)), ((), ())), preferred_element_type=jnp.float32
     )
-    neg_part = jnp.take_along_axis(all_scores, pos, axis=1)
+    cols = lax.broadcasted_iota(jnp.int32, (1, 1, total), 2)
+    neg_part = jnp.sum(jnp.where(pos[:, :, None] == cols, all_scores[:, None, :], 0.0), axis=2)
     pos_part = jnp.sum(query_f * docs_f, axis=1)
     partial_value = jnp.concatenate([pos_part[:, None], neg_part], axis=1)
     scores = ring_sum(partial_value, "mp") / TAU
@@ -139,19 +174,19 @@
     wts = LOSS_SCALE * (prob - first) / TAU
     wts_neg_t = wts[:, 1:].T
     neg_count = pos.shape[1]
-    packed = jnp.concatenate([wts[:, 1:], pos.astype(jnp.float32)], axis=1)
-    packed_all_t = gather_dp(packed).reshape(total, -1).T
+    doc_ids = neg_owner * pairs_here + neg_local
+    packed = jnp.concatenate([wts[:, 1:], doc_ids.astype(jnp.float32)], axis=1)
+    packed_all_t = jnp.stack(gather_rel(packed)).reshape(total, -1).T
     wts_all_t = packed_all_t[:neg_count]
-    pos_all_t = packed_all_t[neg_count:].astype(jnp.int32)
-
-    cols = lax.broadcasted_iota(jnp.int32, (1, 1, total), 2)
+    ids_all_t = packed_all_t[neg_count:].astype(jnp.int32)
+
     coef_q = jnp.sum(jnp.where(pos_t[:, :, None] == cols, wts_neg_t[:, :, None], 0.0), axis=0)
     both = mm(split_bf16(coef_q), e_all)
     grad_query = wts[:, 0:1] * docs_f + both[:pairs_here] + both[pairs_here:]
 
-    me = (lax.axis_index("c") * n_z + lax.axis_index("z")) * n_x + lax.axis_index("x")
+    me = (lax.axis_index("x") * n_z + lax.axis_index("z")) * n_c + lax.axis_index("c")
     own = me * pairs_here + lax.broadcasted_iota(jnp.int32, (1, pairs_here, 1), 1)
-    coef_d = jnp.sum(jnp.where(pos_all_t[:, None, :] == own, wts_all_t[:, None, :], 0.0), axis=0)
+    coef_d = jnp.sum(jnp.where(ids_all_t[:, None, :] == own, wts_all_t[:, None, :], 0.0), axis=0)
     both_d = mm(split_bf16(coef_d), q_all)
     grad_docs = wts[:, 0:1] * query_f + both_d[:pairs_here] + both_d[pairs_here:]
 

time: 470 us -> 450 us (0.957)
  local copies, waits for them, and re-layouts: 85.5 us -> 30.9 us
  waiting for transfers between devices: 215 us -> 236 us
  other arithmetic: 22.4 us -> 35.7 us
    ppermute x6 -> x25, waiting for transfers between devices: 12 us -> 105 us  [the longest x11 78.4 us: ring_blocks(): left = lax.ppermute(left, name, fwd)]
    ppermute x31 -> x20, waiting for transfers between devices: 132 us -> 58.6 us  [ring_collect(): left = lax.ppermute(left, name, fwd)]
    ppermute x6 -> x25, starting transfers between devices: 38.3 us -> 62.5 us  [the longest x8 22.9 us: ring_blocks(): right = lax.ppermute(right, name, bwd)]
    ppermute x20 -> x12, starting transfers between devices: 55 us -> 32.2 us  [ring_collect(): right = lax.ppermute(right, name, bwd)]
    gather x3 -> x0, local copies, waits for them, and re-layouts: 15.7 us -> none  [shards(): neg_part = jnp.take_along_axis(all_scores, pos, axis=1)]
    broadcast_in_dim x12 -> x6, local copies, waits for them, and re-layouts: 13.3 us -> 0.4 us  [ring_collect(): out = jnp.zeros((n,) + v.shape, v.dtype)]
    dynamic_update_slice x4 -> x0, local copies, waits for them, and re-layouts: 11.3 us -> none  [ring_collect(): lax.dynamic_update_index_in_dim(out, lax.ppermute(v, name, fwd), 1 - me, 0)]
    dynamic_update_slice x13 -> x7, local copies, waits for them, and re-layouts: 12.1 us -> 1.2 us  [ring_collect(): out = lax.dynamic_update_index_in_dim(out, v, me, 0)]
  transfers between devices with their start and end apart: 71 -> 71, of which waited for: 43 -> 43; matrix products, arithmetic and copies ran while one was open for 11% -> 7% of each run, Pallas kernels for 0% -> 0%
where the time goes in v5:
time: 450 us; the launch traced here: 441 us
  waiting for transfers between devices  236 us (52%)
  starting transfers between devices  119 us (26%)
  other arithmetic  35.7 us (8%)
  local copies, waits for them, and re-layouts  30.9 us (7%)
  matrix products  18.1 us (4%)
    ppermute x11, waiting for transfers between devices, ring_blocks(): left = lax.ppermute(left, name, fwd)  78.4 us
    ppermute x8, waiting for transfers between devices, ring_reduce(): acc_f = lax.ppermute(acc_f, name, fwd) + block(me + n_fwd - step)  64.3 us
    ppermute x20, waiting for transfers between devices, ring_collect(): left = lax.ppermute(left, name, fwd)  58.6 us
    ppermute x12, starting transfers between devices, ring_collect(): right = lax.ppermute(right, name, bwd)  32.2 us
    ppermute x8, starting transfers between devices, ring_blocks(): right = lax.ppermute(right, name, bwd)  22.9 us
    ppermute x2, starting transfers between devices, ring_blocks(): return [v, lax.ppermute(v, name, fwd)]  19.3 us
    ppermute x2, starting transfers between devices, ring_collect(): pair = jnp.stack([v, lax.ppermute(v, name, fwd)])  17.2 us
    dot_general x3, matrix products, mm(): return jnp.dot(a, b, preferred_element_type=jnp.float32)  12.9 us
  transfers between devices with their start and end apart: 71, of which 43 were waited for; matrix products, arithmetic and copies ran while one was open for 7% of the time, Pallas kernels for 0%

profile of v5, /device:TPU:1, one launch (start us, length us, event | category | flops | bytes accessed | tf_op | source)
XLA Modules:
  0.0 441.3 jit_solution(10198227771240748274)
XLA Ops:
  33.5 8.3 %collective-permute-done.9 = bf16[4,64,512]{2,1,0:T(8,128)(2,1)S(1)} collective-permute-done((bf16[4,64,512]{2,1,0:T(8,128)(2,1)S(1)}, bf16[4,64,512]{2,1,0:T(8,128)(2,1)S(1)}, u32[]{:S(2)}, u32[]{:S(2)}) %collective-permute-start.9) | collective-permute-done | bytes 262176 | tf_op jit(solution)/shard_map/ppermute | solution.py:30
  41.7 7.4 %collective-permute-start.10 = (bf16[8,4,64,512]{3,2,0,1:T(8,128)(2,1)S(1)}, bf16[8,4,64,512]{3,2,0,1:T(8,128)(2,1)}, u32[]{:S(2)}, u32[]{:S(2)}) collective-permute-start(bf16[8,4,64,512]{3,2,0,1:T(8,128)(2,1)S(1)} %bitcast_dynamic-update-slice_fusion.14), channel_id=1, source_target_pairs={{0,4},{4,0},{1,5},{5,1},{2,6},{6,2},{3,7},{7,3},{8,12},{12,8},{9,1... | collective-permute-start | bytes 6291464 | tf_op jit(solution)/shard_map/ppermute | solution.py:23
  63.2 11.4 %collective-permute-done.11 = f32[128,1024]{1,0:T(8,128)S(1)} collective-permute-done((f32[128,1024]{1,0:T(8,128)}, f32[128,1024]{1,0:T(8,128)S(1)}, u32[]{:S(2)}, u32[]{:S(2)}) %collective-permute-start.11) | collective-permute-done | bytes 524320 | tf_op jit(solution)/shard_map/ppermute | solution.py:102
  75.0 13.2 %collective-permute-done.12 = f32[128,1024]{1,0:T(8,128)S(1)} collective-permute-done((f32[128,1024]{1,0:T(8,128)S(1)}, f32[128,1024]{1,0:T(8,128)S(1)}, u32[]{:S(2)}, u32[]{:S(2)}) %collective-permute-start.12) | collective-permute-done | bytes 524320 | tf_op jit(solution)/shard_map/ppermute | solution.py:102
  103.7 7.5 %collective-permute-done.19 = bf16[128,1024]{1,0:T(8,128)(2,1)S(1)} collective-permute-done((bf16[128,1024]{1,0:T(8,128)(2,1)S(1)}, bf16[128,1024]{1,0:T(8,128)(2,1)S(1)}, u32[]{:S(2)}, u32[]{:S(2)}) %collective-permute-start.19) | collective-permute-done | bytes 262176 | tf_op jit(solution)/shard_map/ppermute | solution.py:66
  114.0 16.6 %collective-permute-done.23 = bf16[4,128,1024]{2,1,0:T(8,128)(2,1)S(1)} collective-permute-done((bf16[4,128,1024]{2,1,0:T(8,128)(2,1)S(1)}, bf16[4,128,1024]{2,1,0:T(8,128)(2,1)S(1)}, u32[]{:S(2)}, u32[]{:S(2)}) %collective-permute-start.23) | collective-permute-done | bytes 1048608 | tf_op jit(solution)/shard_map/ppermute | solution.py:66
  133.3 18.9 %collective-permute-done.24 = bf16[4,128,1024]{2,1,0:T(8,128)(2,1)S(1)} collective-permute-done((bf16[4,128,1024]{2,1,0:T(8,128)(2,1)S(1)}, bf16[4,128,1024]{2,1,0:T(8,128)(2,1)S(1)}, u32[]{:S(2)}, u32[]{:S(2)}) %collective-permute-start.24) | collective-permute-done | bytes 1048608 | tf_op jit(solution)/shard_map/ppermute | solution.py:66
  157.3 16.6 %collective-permute-done.25 = bf16[4,128,1024]{2,1,0:T(8,128)(2,1)S(1)} collective-permute-done((bf16[4,128,1024]{2,1,0:T(8,128)(2,1)S(1)}, bf16[4,128,1024]{2,1,0:T(8,128)(2,1)S(1)}, u32[]{:S(2)}, u32[]{:S(2)}) %collective-permute-start.25) | collective-permute-done | bytes 1048608 | tf_op jit(solution)/shard_map/ppermute | solution.py:66
  178.9 9.1 %collective-permute-done.26 = bf16[2,128,1024]{2,1,0:T(8,128)(2,1)S(1)} collective-permute-done((bf16[2,128,1024]{2,1,0:T(8,128)(2,1)S(1)}, bf16[2,128,1024]{2,1,0:T(8,128)(2,1)S(1)}, u32[]{:S(2)}, u32[]{:S(2)}) %collective-permute-start.26) | collective-permute-done | bytes 524320 | tf_op jit(solution)/shard_map/ppermute | solution.py:63
  192.4 10.3 %collective-permute-start.28 = (bf16[8,4,128,1024]{3,2,1,0:T(8,128)(2,1)}, bf16[8,4,128,1024]{3,2,1,0:T(8,128)(2,1)}, u32[]{:S(2)}, u32[]{:S(2)}) collective-permute-start(bf16[8,4,128,1024]{3,2,1,0:T(8,128)(2,1)} %bitcast_dynamic-update-slice_fusion), channel_id=1, source_target_pairs={{0,4},{4,0},{1,5},{5,1},{2,6},{6,2},{3,7},{7,3},{8,12},{12,8},{9,1... | collective-permute-start | bytes 25165832 | tf_op jit(solution)/shard_map/ppermute | solution.py:53
  206.9 8.9 %collective-permute-done.28 = bf16[8,4,128,1024]{3,2,1,0:T(8,128)(2,1)} collective-permute-done((bf16[8,4,128,1024]{3,2,1,0:T(8,128)(2,1)}, bf16[8,4,128,1024]{3,2,1,0:T(8,128)(2,1)}, u32[]{:S(2)}, u32[]{:S(2)}) %collective-permute-start.28) | collective-permute-done | bytes 8388640 | tf_op jit(solution)/shard_map/ppermute | solution.py:53
  227.4 4.5 %select_reduce_fusion.2 = f32[64,31]{0,1:T(8,128)S(1)} fusion(f32[64,4096]{1,0:T(8,128)S(1)} %fusion.18, s32[64,31]{0,1:T(8,128)S(1)} %get-tuple-element.35), kind=kLoop, calls=%fused_computation.3 | loop fusion | flops 24377408 | bytes 1064448 | tf_op jit(solution)/shard_map/reduce_sum | solution.py:167
  242.5 5.5 %select_reduce_fusion.1 = f32[64,4096]{1,0:T(8,128)S(1)} fusion(f32[31,64]{1,0:T(8,128)S(1)} %get-tuple-element.37, s32[31,64]{1,0:T(8,128)S(1)} %bitcast.249), kind=kLoop, calls=%fused_computation.1 | loop fusion | flops 24117248 | bytes 1064448 | tf_op jit(solution)/shard_map/reduce_sum | solution.py:183
  267.0 5.8 %collective-permute-done.40 = f32[4,64,62]{1,2,0:T(8,128)S(1)} collective-permute-done((f32[4,64,62]{1,2,0:T(8,128)S(1)}, f32[4,64,62]{1,2,0:T(8,128)S(1)}, u32[]{:S(2)}, u32[]{:S(2)}) %collective-permute-start.40) | collective-permute-done | bytes 63520 | tf_op jit(solution)/shard_map/ppermute | solution.py:66
  272.8 5.0 %collective-permute-done.41 = f32[4,64,62]{1,2,0:T(8,128)S(1)} collective-permute-done((f32[4,64,62]{1,2,0:T(8,128)S(1)}, f32[4,64,62]{1,2,0:T(8,128)S(1)}, u32[]{:S(2)}, u32[]{:S(2)}) %collective-permute-start.41) | collective-permute-done | bytes 63520 | tf_op jit(solution)/shard_map/ppermute | solution.py:66
  278.5 8.9 %collective-permute-start.42 = (f32[8,4,64,62]{2,0,3,1:T(8,128)S(1)}, f32[8,4,64,62]{2,0,3,1:T(8,128)S(1)}, u32[]{:S(2)}, u32[]{:S(2)}) collective-permute-start(f32[8,4,64,62]{2,0,3,1:T(8,128)S(1)} %copy.143), channel_id=1, source_target_pairs={{0,4},{4,0},{1,5},{5,1},{2,6},{6,2},{3,7},{7,3},{8,12},{12,8},{9,1... | collective-permute-start | bytes 1523720 | tf_op jit(solution)/shard_map/ppermute | solution.py:53
  287.4 4.7 %fusion.1 = f32[128,1024]{1,0:T(8,128)S(1)} fusion(bf16[4096,1024]{1,0:T(8,128)(2,1)} %bitcast.228, bf16[64,4096]{1,0:T(8,128)(2,1)S(1)} %get-tuple-element.3, bf16[64,4096]{1,0:T(8,128)(2,1)S(1)} %get-tuple-element.4), kind=kOutput, calls=%fused_computation.20 | convolution fusion | flops 1075838976 | bytes 9961472 | tf_op jit(solution)/shard_map/dot_general | solution.py:123
  301.8 4.6 %fusion.5 = f32[128,1024]{1,0:T(8,128)S(1)} fusion(bf16[4096,1024]{1,0:T(8,128)(2,1)} %bitcast.233, bf16[64,4096]{1,0:T(8,128)(2,1)S(1)} %get-tuple-element.5, bf16[64,4096]{1,0:T(8,128)(2,1)S(1)} %get-tuple-element.6), kind=kOutput, calls=%fused_computation.24 | convolution fusion | flops 1075838976 | bytes 9961472 | tf_op jit(solution)/shard_map/dot_general | solution.py:123
  322.2 5.8 %collective-permute-done.48 = bf16[128,1024]{1,0:T(8,128)(2,1)S(1)} collective-permute-done((bf16[128,1024]{1,0:T(8,128)(2,1)S(1)}, bf16[128,1024]{1,0:T(8,128)(2,1)S(1)}, u32[]{:S(2)}, u32[]{:S(2)}) %collective-permute-start.48) | collective-permute-done | bytes 262176 | tf_op jit(solution)/shard_map/ppermute | solution.py:30
  338.3 7.1 %collective-permute-done.49 = f32[4,8,64,512]{3,2,1,0:T(8,128)} collective-permute-done((f32[4,8,64,512]{3,2,1,0:T(8,128)}, f32[4,8,64,512]{3,2,1,0:T(8,128)}, u32[]{:S(2)}, u32[]{:S(2)}) %collective-permute-start.49) | collective-permute-done | bytes 4194336 | tf_op jit(solution)/shard_map/ppermute | solution.py:97
  352.7 11.6 %collective-permute-done.50 = f32[4,64,512]{2,1,0:T(8,128)S(1)} collective-permute-done((f32[4,64,512]{2,1,0:T(8,128)S(1)}, f32[4,64,512]{2,1,0:T(8,128)S(1)}, u32[]{:S(2)}, u32[]{:S(2)}) %collective-permute-start.50) | collective-permute-done | bytes 524320 | tf_op jit(solution)/shard_map/ppermute | solution.py:102
  364.6 13.4 %collective-permute-done.51 = f32[4,64,512]{2,1,0:T(8,128)S(1)} collective-permute-done((f32[4,64,512]{2,1,0:T(8,128)S(1)}, f32[4,64,512]{2,1,0:T(8,128)S(1)}, u32[]{:S(2)}, u32[]{:S(2)}) %collective-permute-start.51) | collective-permute-done | bytes 524320 | tf_op jit(solution)/shard_map/ppermute | solution.py:102
  381.0 9.9 %collective-permute-done.52 = f32[4,64,512]{2,1,0:T(8,128)S(1)} collective-permute-done((f32[4,64,512]{2,1,0:T(8,128)S(1)}, f32[4,64,512]{2,1,0:T(8,128)S(1)}, u32[]{:S(2)}, u32[]{:S(2)}) %collective-permute-start.52) | collective-permute-done | bytes 524320 | tf_op jit(solution)/shard_map/ppermute | solution.py:102
  417.7 9.7 %collective-permute-start.70 = (f32[8,4,1024]{2,0,1:T(8,128)S(1)}, f32[8,4,1024]{2,0,1:T(8,128)S(1)}, u32[]{:S(2)}, u32[]{:S(2)}) collective-permute-start(f32[8,4,1024]{2,0,1:T(8,128)S(1)} %dynamic_update_slice.166), channel_id=1, source_target_pairs={{0,4},{4,0},{1,5},{5,1},{2,6},{6,2},{3,7},{7,3},{8,12},{12,8},{9,1... | collective-permute-start | bytes 393224 | tf_op jit(solution)/shard_map/ppermute | solution.py:23
  (275 shorter events, 214.3 us)
Async XLA Ops:
  10.2 9.6 %collective-permute-start.3 = (bf16[4,64,512]{2,1,0:T(8,128)(2,1)S(1)}, bf16[4,64,512]{2,1,0:T(8,128)(2,1)S(1)}, u32[]{:S(2)}, u32[]{:S(2)}) collective-permute-start(bf16[4,64,512]{2,1,0:T(8,128)(2,1)S(1)} %bitcast_dynamic-update-slice_fusion.23), channel_id=1, source_target_pairs={{0,8},{8,16},{16,24},{24,32},{32,40},{40,48},{48,56},{56,0},{1,9},... | collective-permute-start | bytes 786440 | tf_op jit(solution)/shard_map/ppermute | solution.py:40
  41.7 11.4 %collective-permute-start.10 = (bf16[8,4,64,512]{3,2,0,1:T(8,128)(2,1)S(1)}, bf16[8,4,64,512]{3,2,0,1:T(8,128)(2,1)}, u32[]{:S(2)}, u32[]{:S(2)}) collective-permute-start(bf16[8,4,64,512]{3,2,0,1:T(8,128)(2,1)S(1)} %bitcast_dynamic-update-slice_fusion.14), channel_id=1, source_target_pairs={{0,4},{4,0},{1,5},{5,1},{2,6},{6,2},{3,7},{7,3},{8,12},{12,8},{9,1... | collective-permute-start | bytes 6291464 | tf_op jit(solution)/shard_map/ppermute | solution.py:23
  59.6 15.0 %collective-permute-start.11 = (f32[128,1024]{1,0:T(8,128)}, f32[128,1024]{1,0:T(8,128)S(1)}, u32[]{:S(2)}, u32[]{:S(2)}) collective-permute-start(f32[128,1024]{1,0:T(8,128)} %bitcast.28), channel_id=1, source_target_pairs={{0,1},{1,2},{2,3},{3,0},{4,5},{5,6},{6,7},{7,4},{8,9},{9,10},{10,1... | collective-permute-start | bytes 1572872 | tf_op jit(solution)/shard_map/ppermute | solution.py:102
  61.7 13.4 %collective-permute-start.13 = (f32[128,1024]{1,0:T(8,128)S(1)}, f32[128,1024]{1,0:T(8,128)}, u32[]{:S(2)}, u32[]{:S(2)}) collective-permute-start(f32[128,1024]{1,0:T(8,128)S(1)} %bitcast.244), channel_id=1, source_target_pairs={{0,3},{1,0},{2,1},{3,2},{4,7},{5,4},{6,5},{7,6},{8,11},{9,8},{10,9... | collective-permute-start | bytes 1572872 | tf_op jit(solution)/shard_map/ppermute | solution.py:108
  74.7 13.6 %collective-permute-start.12 = (f32[128,1024]{1,0:T(8,128)S(1)}, f32[128,1024]{1,0:T(8,128)S(1)}, u32[]{:S(2)}, u32[]{:S(2)}) collective-permute-start(f32[128,1024]{1,0:T(8,128)S(1)} %bitcast_add_fusion.8), channel_id=1, source_target_pairs={{0,1},{1,2},{2,3},{3,0},{4,5},{5,6},{6,7},{7,4},{8,9},{9,10},{10,1... | collective-permute-start | bytes 1572872 | tf_op jit(solution)/shard_map/ppermute | solution.py:102
  111.3 19.4 %collective-permute-start.23 = (bf16[4,128,1024]{2,1,0:T(8,128)(2,1)S(1)}, bf16[4,128,1024]{2,1,0:T(8,128)(2,1)S(1)}, u32[]{:S(2)}, u32[]{:S(2)}) collective-permute-start(bf16[4,128,1024]{2,1,0:T(8,128)(2,1)S(1)} %pad_maximum_fusion.4), channel_id=1, source_target_pairs={{0,8},{8,16},{16,24},{24,32},{32,40},{40,48},{48,56},{56,0},{1,9},... | collective-permute-start | bytes 3145736 | tf_op jit(solution)/shard_map/ppermute | solution.py:66
  111.4 19.3 %collective-permute-start.20 = (bf16[4,128,1024]{2,1,0:T(8,128)(2,1)S(1)}, bf16[4,128,1024]{2,1,0:T(8,128)(2,1)S(1)}, u32[]{:S(2)}, u32[]{:S(2)}) collective-permute-start(bf16[4,128,1024]{2,1,0:T(8,128)(2,1)S(1)} %pad_maximum_fusion.4), channel_id=1, source_target_pairs={{0,56},{8,0},{16,8},{24,16},{32,24},{40,32},{48,40},{56,48},{1,57}... | collective-permute-start | bytes 3145736 | tf_op jit(solution)/shard_map/ppermute | solution.py:69
  130.7 21.6 %collective-permute-start.24 = (bf16[4,128,1024]{2,1,0:T(8,128)(2,1)S(1)}, bf16[4,128,1024]{2,1,0:T(8,128)(2,1)S(1)}, u32[]{:S(2)}, u32[]{:S(2)}) collective-permute-start(bf16[4,128,1024]{2,1,0:T(8,128)(2,1)S(1)} %collective-permute-done.23), channel_id=1, source_target_pairs={{0,8},{8,16},{16,24},{24,32},{32,40},{40,48},{48,56},{56,0},{1,9},... | collective-permute-start | bytes 3145736 | tf_op jit(solution)/shard_map/ppermute | solution.py:66
  130.7 21.6 %collective-permute-start.21 = (bf16[4,128,1024]{2,1,0:T(8,128)(2,1)S(1)}, bf16[4,128,1024]{2,1,0:T(8,128)(2,1)S(1)}, u32[]{:S(2)}, u32[]{:S(2)}) collective-permute-start(bf16[4,128,1024]{2,1,0:T(8,128)(2,1)S(1)} %collective-permute-done.20), channel_id=1, source_target_pairs={{0,56},{8,0},{16,8},{24,16},{32,24},{40,32},{48,40},{56,48},{1,57}... | collective-permute-start | bytes 3145736 | tf_op jit(solution)/shard_map/ppermute | solution.py:69
  152.3 21.6 %collective-permute-start.25 = (bf16[4,128,1024]{2,1,0:T(8,128)(2,1)S(1)}, bf16[4,128,1024]{2,1,0:T(8,128)(2,1)S(1)}, u32[]{:S(2)}, u32[]{:S(2)}) collective-permute-start(bf16[4,128,1024]{2,1,0:T(8,128)(2,1)S(1)} %collective-permute-done.24), channel_id=1, source_target_pairs={{0,8},{8,16},{16,24},{24,32},{32,40},{40,48},{48,56},{56,0},{1,9},... | collective-permute-start | bytes 3145736 | tf_op jit(solution)/shard_map/ppermute | solution.py:66
  152.3 21.7 %collective-permute-start.22 = (bf16[4,128,1024]{2,1,0:T(8,128)(2,1)S(1)}, bf16[4,128,1024]{2,1,0:T(8,128)(2,1)S(1)}, u32[]{:S(2)}, u32[]{:S(2)}) collective-permute-start(bf16[4,128,1024]{2,1,0:T(8,128)(2,1)S(1)} %collective-permute-done.21), channel_id=1, source_target_pairs={{0,56},{8,0},{16,8},{24,16},{32,24},{40,32},{48,40},{56,48},{1,57}... | collective-permute-start | bytes 3145736 | tf_op jit(solution)/shard_map/ppermute | solution.py:69
  173.9 14.1 %collective-permute-start.26 = (bf16[2,128,1024]{2,1,0:T(8,128)(2,1)S(1)}, bf16[2,128,1024]{2,1,0:T(8,128)(2,1)S(1)}, u32[]{:S(2)}, u32[]{:S(2)}) collective-permute-start(bf16[2,128,1024]{2,1,0:T(8,128)(2,1)S(1)} %slice.68), channel_id=1, source_target_pairs={{0,8},{8,16},{16,24},{24,32},{32,40},{40,48},{48,56},{56,0},{1,9},... | collective-permute-start | bytes 1572872 | tf_op jit(solution)/shard_map/ppermute | solution.py:63
  174.1 13.9 %collective-permute-start.27 = (bf16[2,128,1024]{2,1,0:T(8,128)(2,1)S(1)}, bf16[2,128,1024]{2,1,0:T(8,128)(2,1)S(1)}, u32[]{:S(2)}, u32[]{:S(2)}) collective-permute-start(bf16[2,128,1024]{2,1,0:T(8,128)(2,1)S(1)} %slice.69), channel_id=1, source_target_pairs={{0,56},{8,0},{16,8},{24,16},{32,24},{40,32},{48,40},{56,48},{1,57}... | collective-permute-start | bytes 1572872 | tf_op jit(solution)/shard_map/ppermute | solution.py:63
  192.4 23.5 %collective-permute-start.28 = (bf16[8,4,128,1024]{3,2,1,0:T(8,128)(2,1)}, bf16[8,4,128,1024]{3,2,1,0:T(8,128)(2,1)}, u32[]{:S(2)}, u32[]{:S(2)}) collective-permute-start(bf16[8,4,128,1024]{3,2,1,0:T(8,128)(2,1)} %bitcast_dynamic-update-slice_fusion), channel_id=1, source_target_pairs={{0,4},{4,0},{1,5},{5,1},{2,6},{6,2},{3,7},{7,3},{8,12},{12,8},{9,1... | collective-permute-start | bytes 25165832 | tf_op jit(solution)/shard_map/ppermute | solution.py:53
  278.5 13.7 %collective-permute-start.42 = (f32[8,4,64,62]{2,0,3,1:T(8,128)S(1)}, f32[8,4,64,62]{2,0,3,1:T(8,128)S(1)}, u32[]{:S(2)}, u32[]{:S(2)}) collective-permute-start(f32[8,4,64,62]{2,0,3,1:T(8,128)S(1)} %copy.143), channel_id=1, source_target_pairs={{0,4},{4,0},{1,5},{5,1},{2,6},{6,2},{3,7},{7,3},{8,12},{12,8},{9,1... | collective-permute-start | bytes 1523720 | tf_op jit(solution)/shard_map/ppermute | solution.py:53
  333.9 11.4 %collective-permute-start.49 = (f32[4,8,64,512]{3,2,1,0:T(8,128)}, f32[4,8,64,512]{3,2,1,0:T(8,128)}, u32[]{:S(2)}, u32[]{:S(2)}) collective-permute-start(f32[4,8,64,512]{3,2,1,0:T(8,128)} %dynamic-slice_bitcast_fusion), channel_id=1, source_target_pairs={{0,4},{4,0},{1,5},{5,1},{2,6},{6,2},{3,7},{7,3},{8,12},{12,8},{9,1... | collective-permute-start | bytes 12582920 | tf_op jit(solution)/shard_map/ppermute | solution.py:97
  350.0 14.4 %collective-permute-start.50 = (f32[4,64,512]{2,1,0:T(8,128)S(1)}, f32[4,64,512]{2,1,0:T(8,128)S(1)}, u32[]{:S(2)}, u32[]{:S(2)}) collective-permute-start(f32[4,64,512]{2,1,0:T(8,128)S(1)} %get-tuple-element.19), channel_id=1, source_target_pairs={{0,8},{8,16},{16,24},{24,32},{32,40},{40,48},{48,56},{56,0},{1,9},... | collective-permute-start | bytes 1572872 | tf_op jit(solution)/shard_map/ppermute | solution.py:102
  350.1 14.5 %collective-permute-start.54 = (f32[4,64,512]{2,1,0:T(8,128)S(1)}, f32[4,64,512]{2,1,0:T(8,128)S(1)}, u32[]{:S(2)}, u32[]{:S(2)}) collective-permute-start(f32[4,64,512]{2,1,0:T(8,128)S(1)} %get-tuple-element.20), channel_id=1, source_target_pairs={{0,56},{8,0},{16,8},{24,16},{32,24},{40,32},{48,40},{56,48},{1,57}... | collective-permute-start | bytes 1572872 | tf_op jit(solution)/shard_map/ppermute | solution.py:107
  364.5 13.5 %collective-permute-start.51 = (f32[4,64,512]{2,1,0:T(8,128)S(1)}, f32[4,64,512]{2,1,0:T(8,128)S(1)}, u32[]{:S(2)}, u32[]{:S(2)}) collective-permute-start(f32[4,64,512]{2,1,0:T(8,128)S(1)} %bitcast_add_fusion.6), channel_id=1, source_target_pairs={{0,8},{8,16},{16,24},{24,32},{32,40},{40,48},{48,56},{56,0},{1,9},... | collective-permute-start | bytes 1572872 | tf_op jit(solution)/shard_map/ppermute | solution.py:102
  378.2 12.7 %collective-permute-start.52 = (f32[4,64,512]{2,1,0:T(8,128)S(1)}, f32[4,64,512]{2,1,0:T(8,128)S(1)}, u32[]{:S(2)}, u32[]{:S(2)}) collective-permute-start(f32[4,64,512]{2,1,0:T(8,128)S(1)} %get-tuple-element.17), channel_id=1, source_target_pairs={{0,8},{8,16},{16,24},{24,32},{32,40},{40,48},{48,56},{56,0},{1,9},... | collective-permute-start | bytes 1572872 | tf_op jit(solution)/shard_map/ppermute | solution.py:102
  378.3 12.6 %collective-permute-start.55 = (f32[4,64,512]{2,1,0:T(8,128)S(1)}, f32[4,64,512]{2,1,0:T(8,128)S(1)}, u32[]{:S(2)}, u32[]{:S(2)}) collective-permute-start(f32[4,64,512]{2,1,0:T(8,128)S(1)} %get-tuple-element.18), channel_id=1, source_target_pairs={{0,56},{8,0},{16,8},{24,16},{32,24},{40,32},{48,40},{56,48},{1,57}... | collective-permute-start | bytes 1572872 | tf_op jit(solution)/shard_map/ppermute | solution.py:107
  391.1 36.2 %collective-permute-start.53 = (f32[4,64,512]{2,1,0:T(8,128)S(1)}, f32[4,64,512]{2,1,0:T(8,128)S(1)}, u32[]{:S(2)}, u32[]{:S(2)}) collective-permute-start(f32[4,64,512]{2,1,0:T(8,128)S(1)} %get-tuple-element.15), channel_id=1, source_target_pairs={{0,8},{8,16},{16,24},{24,32},{32,40},{40,48},{48,56},{56,0},{1,9},... | collective-permute-start | bytes 1572872 | tf_op jit(solution)/shard_map/ppermute | solution.py:102
  391.2 36.1 %collective-permute-start.56 = (f32[4,64,512]{2,1,0:T(8,128)S(1)}, f32[4,64,512]{2,1,0:T(8,128)S(1)}, u32[]{:S(2)}, u32[]{:S(2)}) collective-permute-start(f32[4,64,512]{2,1,0:T(8,128)S(1)} %get-tuple-element.16), channel_id=1, source_target_pairs={{0,56},{8,0},{16,8},{24,16},{32,24},{40,32},{48,40},{56,48},{1,57}... | collective-permute-start | bytes 1572872 | tf_op jit(solution)/shard_map/ppermute | solution.py:108
  417.7 11.0 %collective-permute-start.70 = (f32[8,4,1024]{2,0,1:T(8,128)S(1)}, f32[8,4,1024]{2,0,1:T(8,128)S(1)}, u32[]{:S(2)}, u32[]{:S(2)}) collective-permute-start(f32[8,4,1024]{2,0,1:T(8,128)S(1)} %dynamic_update_slice.166), channel_id=1, source_target_pairs={{0,4},{4,0},{1,5},{5,1},{2,6},{6,2},{3,7},{7,3},{8,12},{12,8},{9,1... | collective-permute-start | bytes 393224 | tf_op jit(solution)/shard_map/ppermute | solution.py:23
  (56 other events, 471.6 us)
